TPU v7x, 256 devices: a whole 4x4x8 slice. The times are simulated.
256 devices in a mesh: section: 2 (over core), shard: 128 (over z, x, y).
Axes of the slice: x: 4, y: 4, z: 8, core: 2. Of those that a mesh axis runs over, the one named last changes fastest.
Arguments:
- hidden: bfloat16 [512, 32, 768], P('shard', None, 'section'), may hold values from -6 to 6
- proj: bfloat16 [768, 128], P('section'), may hold values from -0.21875 to 0.21875
- passages: bfloat16 [16384, 180, 128], P('shard'), may hold values from -24 to 24
- pass_len: int32 [16384], P('shard'), may hold values from 45 to 180
- query_len: int32 [512], P('shard'), may hold values from 8 to 32
- cand_owner: int32 [2, 512, 32, 1], P('section', 'shard'), may hold values from 0 to 127; in each aligned block of 128 rows (0 to 127, 128 to 255, ..., all dimensions but the last counted through in order) at most 2 rows name the same one
- cand_slot: int32 [2, 512, 32], P('section', 'shard'), may hold values from 0 to 127
- teacher: float32 [512, 64], P('shard', 'section'), may hold values from -18 to 318
Outputs:
- kl_div: float32 [512], P('shard')
- grad_hidden: bfloat16 [512, 32, 768], P('shard', None, 'section')
- grad_proj: float32 [768, 128], P('section')
Inputs may be any that keep to these rules, and one draw needn't show every extreme that they name: `cand_owner`: among the 128 candidates held by one device (one index of section, the queries of one index of shard), at most 2 name any one owner.
All inputs are finite; a program needn't handle non-finite values.
Results may differ from a plain program's by a relative error of at most 0.022.
Values may be sent and summed in bfloat16 or wider, within the bound.
No kernel may reach another device: no remote copies, remote signals or barrier semaphores. Data moves between devices by JAX's collectives and lax.ppermute only.
A program may use at most 128 MiB of HBM per device.

v0:
```python
import jax
import jax.numpy as jnp
from jax import lax
from jax.sharding import PartitionSpec as P
from jax.experimental import pallas as pl
from jax.experimental.pallas import tpu as pltpu

SHARPNESS = 64.0
EPSILON = 1e-06
NEGATIVE = -1e30
CAPACITY = 2
GROUP = 8


def combined_all(value, axis, join):
    pieces = jax.tree.map(lambda part: lax.all_gather(part, axis), value)
    head = jax.tree.map(lambda part: part[0], pieces)
    tail = jax.tree.map(lambda part: part[1:], pieces)
    running, _ = lax.scan(lambda running, section: (join(running, section), None), head, tail)
    return running


def token_scores(q_rows, blocks, cand_lens):
    logits = (
        jnp.einsum("bid,btd->bit", q_rows, blocks, preferred_element_type=jnp.float32) * SHARPNESS
    )
    in_range = jnp.arange(blocks.shape[1])[None, None, :] < cand_lens[:, None, None]
    logits = jnp.where(in_range, logits, NEGATIVE)
    top_logit = jnp.max(logits, axis=2, keepdims=True)
    expo_terms = jnp.where(in_range, jnp.exp(logits - top_logit), 0.0)
    total = jnp.sum(expo_terms, axis=2, keepdims=True)
    token_max = (top_logit[..., 0] + jnp.log(total[..., 0])) / SHARPNESS
    return (token_max, expo_terms / total)


def merge_halves(first, second):
    teach_top = jnp.maximum(first[0], second[0])
    scale_one = jnp.exp(first[0] - teach_top)
    scale_two = jnp.exp(second[0] - teach_top)
    stud_top = jnp.maximum(first[3], second[3])
    fact_one = jnp.exp(first[3] - stud_top)
    fact_two = jnp.exp(second[3] - stud_top)
    return (
        teach_top,
        first[1] * scale_one + second[1] * scale_two,
        first[2] * scale_one + second[2] * scale_two,
        stud_top,
        first[4] * fact_one + second[4] * fact_two,
    )


def pair_sum(value):
    return value + lax.ppermute(value, "section", [(0, 1), (1, 0)])


def spread_sum(value, axis, size):
    pieces = value.reshape(size, -1, value.shape[-1])
    summed = lax.all_to_all(pieces, axis, 0, 0, tiled=True).sum(axis=0)
    spread = jnp.broadcast_to(summed[None], pieces.shape)
    return lax.all_to_all(spread, axis, 0, 0, tiled=True).reshape(value.shape)


def split_three(value):
    high = lax.reduce_precision(value, exponent_bits=8, mantissa_bits=7)
    rest = value - high
    middle = lax.reduce_precision(rest, exponent_bits=8, mantissa_bits=7)
    return high, middle, rest - middle


def lane_row(width, entries):
    lane = jnp.arange(width)[None, :]
    row = jnp.zeros((entries[0].shape[0], width), jnp.float32)
    for place, entry in enumerate(entries):
        spots = entry.shape[1]
        for spot in range(spots):
            row = jnp.where(lane == place * spots + spot, entry[:, spot : spot + 1].astype(jnp.float32), row)
    return row.astype(jnp.bfloat16)[:, None, :]


def score_kernel(slot_ref, qlen_ref, len_ref, q_ref, p_ref, pt_ref, pulled_ref, stud_ref):
    group, num_tokens, _ = q_ref.shape
    pass_tokens = p_ref.shape[1]
    base = pl.program_id(0) * group
    for spot in range(group):
        slot = slot_ref[base + spot]
        limit = len_ref[slot]
        logits = (
            lax.dot_general(
                p_ref[slot], q_ref[spot], (((1,), (1,)), ((), ())), preferred_element_type=jnp.float32
            )
            * SHARPNESS
        )
        in_range = lax.broadcasted_iota(jnp.int32, (pass_tokens, num_tokens), 0) < limit
        logits = jnp.where(in_range, logits, NEGATIVE)
        top_logit = jnp.max(logits, axis=0, keepdims=True)
        expo_terms = jnp.where(in_range, jnp.exp(logits - top_logit), 0.0)
        total = jnp.sum(expo_terms, axis=0, keepdims=True)
        token_max = (top_logit + jnp.log(total)) / SHARPNESS
        weight = (expo_terms / total).astype(jnp.bfloat16)
        pulled = jnp.dot(pt_ref[slot], weight, preferred_element_type=jnp.float32)
        pulled_ref[spot] = pulled.T.astype(jnp.bfloat16)
        cols = lax.broadcasted_iota(jnp.int32, (1, num_tokens), 1)
        score = jnp.sum(jnp.where(cols < qlen_ref[base + spot], token_max, 0.0))
        stud_ref[pl.ds(spot, 1), :] = jnp.full((1, stud_ref.shape[1]), score, jnp.float32)


def owner_scores(q_rows, passages, slot_at, qlen_at, pass_len):
    slots, num_tokens, vec_dim = q_rows.shape
    held, pass_tokens, _ = passages.shape
    group = GROUP
    grid_spec = pltpu.PrefetchScalarGridSpec(
        num_scalar_prefetch=3,
        grid=(slots // group,),
        in_specs=[
            pl.BlockSpec((group, num_tokens, vec_dim), lambda i, *_: (i, 0, 0)),
            pl.BlockSpec((held, pass_tokens, vec_dim), lambda i, *_: (0, 0, 0)),
            pl.BlockSpec((held, vec_dim, pass_tokens), lambda i, *_: (0, 0, 0)),
        ],
        out_specs=[
            pl.BlockSpec((group, num_tokens, vec_dim), lambda i, *_: (i, 0, 0)),
            pl.BlockSpec((group, 128), lambda i, *_: (i, 0)),
        ],
    )
    flops = 4 * slots * num_tokens * pass_tokens * vec_dim
    moved = 2 * (2 * held * pass_tokens * vec_dim + 2 * slots * num_tokens * vec_dim)
    return pl.pallas_call(
        score_kernel,
        grid_spec=grid_spec,
        out_shape=[
            jax.ShapeDtypeStruct((slots, num_tokens, vec_dim), jnp.bfloat16),
            jax.ShapeDtypeStruct((slots, 128), jnp.float32),
        ],
        compiler_params=pltpu.CompilerParams(vmem_limit_bytes=60 * 1024 * 1024),
        cost_estimate=pl.CostEstimate(
            flops=flops, transcendentals=slots * num_tokens * pass_tokens, bytes_accessed=moved
        ),
    )(slot_at, qlen_at, pass_len, q_rows, passages, jnp.swapaxes(passages, 1, 2))


def local(hidden, proj, passages, pass_len, query_len, cand_owner, cand_slot, teacher):
    num_queries, num_tokens, feat_half = hidden.shape
    vec_dim = proj.shape[1]
    held = passages.shape[0]
    owners = lax.axis_size("shard")
    flat_h = hidden.reshape(num_queries * num_tokens, feat_half)
    partial_in = jnp.dot(flat_h, proj, preferred_element_type=jnp.float32).reshape(
        num_queries, num_tokens, vec_dim
    )
    proj_in = pair_sum(partial_in)
    inv_norm = lax.rsqrt(jnp.sum(proj_in * proj_in, axis=2, keepdims=True) + EPSILON)
    query_vecs = (proj_in * inv_norm).astype(jnp.bfloat16)
    tok_mask = jnp.arange(num_tokens)[None, :] < query_len[:, None]
    owner_ids = cand_owner.reshape(-1)
    slot_ids = cand_slot.reshape(-1)
    requests = owner_ids.shape[0]
    cand_half = requests // num_queries
    capacity = CAPACITY
    slots = owners * capacity
    onehot = (owner_ids[:, None] == jnp.arange(owners)[None, :]).astype(jnp.int32)
    rank_ids = jnp.sum((jnp.cumsum(onehot, axis=0) - onehot) * onehot, axis=1)
    buf_pos = owner_ids * capacity + rank_ids
    query_of = jnp.arange(requests) // cand_half
    pick = buf_pos[None, :] == jnp.arange(slots)[:, None]
    slot_query = jnp.any(pick[:, :, None] & (query_of[:, None] == jnp.arange(num_queries))[None], axis=1)
    q_send = jnp.einsum(
        "sq,qid->sid", slot_query.astype(jnp.bfloat16), query_vecs, preferred_element_type=jnp.float32
    ).astype(jnp.bfloat16)
    slot_meta = jnp.sum(jnp.where(pick, slot_ids[None, :], 0), axis=1).reshape(owners, capacity)
    qlen_meta = jnp.sum(jnp.where(pick, query_len[query_of][None, :], 0), axis=1).reshape(owners, capacity)
    body = capacity * num_tokens
    payload = jnp.concatenate(
        [q_send.reshape(owners, body, vec_dim), lane_row(vec_dim, (slot_meta, qlen_meta))], axis=1
    )
    recv = lax.all_to_all(payload, "shard", 0, 0, tiled=True)
    q_rows = recv[:, :body, :].reshape(slots, num_tokens, vec_dim)
    slot_at = recv[:, body, :capacity].astype(jnp.int32).reshape(slots)
    qlen_at = recv[:, body, capacity : 2 * capacity].astype(jnp.int32).reshape(slots)
    pulled, stud_rows = owner_scores(q_rows, passages, slot_at, qlen_at, pass_len)
    stud_at = stud_rows[:, 0]
    pieces = tuple(piece.reshape(owners, capacity) for piece in split_three(stud_at))
    back = jnp.concatenate(
        [pulled.reshape(owners, body, vec_dim), lane_row(vec_dim, pieces)], axis=1
    )
    got = lax.all_to_all(back, "shard", 0, 0, tiled=True)
    got_pulled = got[:, :body, :].reshape(slots, num_tokens, vec_dim)
    take = pick.T.astype(jnp.bfloat16)
    mine = jnp.einsum("rs,sid->rid", take, got_pulled, preferred_element_type=jnp.float32)
    got_meta = got[:, body, : 3 * capacity].astype(jnp.float32).reshape(owners, 3, capacity)
    got_meta = jnp.transpose(got_meta, (1, 0, 2)).reshape(3, slots)
    parts = jnp.sum(jnp.where(pick[None], got_meta[:, :, None], 0.0), axis=1)
    student = ((parts[0] + parts[1]) + parts[2]).reshape(num_queries, cand_half)
    pulled_mine = mine.reshape(num_queries, cand_half, num_tokens, vec_dim)
    teach_top = jnp.max(teacher, axis=1)
    teach_exp = jnp.exp(teacher - teach_top[:, None])
    teach_sum = jnp.sum(teach_exp, axis=1)
    teach_wsum = jnp.sum(teach_exp * (teacher - student), axis=1)
    stud_top = jnp.max(student, axis=1)
    stud_sum = jnp.sum(jnp.exp(student - stud_top[:, None]), axis=1)
    top_teach, sum_teach, wsum_teach, top_stud, sum_stud = combined_all(
        (teach_top, teach_sum, teach_wsum, stud_top, stud_sum), "section", merge_halves
    )
    lse_teach = top_teach + jnp.log(sum_teach)
    lse_stud = top_stud + jnp.log(sum_stud)
    kl_div = wsum_teach / sum_teach - lse_teach + lse_stud
    score_grad = jnp.exp(student - lse_stud[:, None]) - jnp.exp(teacher - lse_teach[:, None])
    half_grad = jnp.sum(score_grad[:, :, None, None] * pulled_mine, axis=1)
    half_grad = jnp.where(tok_mask[:, :, None], half_grad, 0.0)
    vec_grad = pair_sum(half_grad)
    cubed = inv_norm * inv_norm * inv_norm
    in_grad = inv_norm * vec_grad - cubed * proj_in * jnp.sum(
        proj_in * vec_grad, axis=2, keepdims=True
    )
    flat_in = in_grad.astype(jnp.bfloat16).reshape(num_queries * num_tokens, vec_dim)
    grad_hidden = jnp.dot(flat_in, proj.T, preferred_element_type=jnp.float32).astype(jnp.bfloat16)
    grad_hidden = grad_hidden.reshape(num_queries, num_tokens, feat_half)
    local_proj = jnp.dot(flat_h.T, flat_in, preferred_element_type=jnp.float32)
    grad_proj = spread_sum(local_proj, "shard", owners)
    return (kl_div, grad_hidden, grad_proj)


def solution(mesh):
    in_specs = (
        P("shard", None, "section"),
        P("section", None),
        P("shard", None, None),
        P("shard"),
        P("shard"),
        P("section", "shard", None, None),
        P("section", "shard", None),
        P("shard", "section"),
    )
    out_specs = (P("shard"), P("shard", None, "section"), P("section", None))
    return jax.shard_map(local, mesh=mesh, in_specs=in_specs, out_specs=out_specs, check_vma=False)
```

profile of v0, /device:TPU:2, one launch (start us, length us, event | category | flops | bytes accessed | tf_op | source)
XLA Modules:
  0.0 264.8 jit_solution(2247620189711295588)
XLA Ops:
  0.6 0.9 copy-done
  1.5 1.1 fusion.7
  2.7 1.5 fusion.28
  4.2 0.5 broadcast.645
  4.7 1.3 broadcast_multiply_fusion
  6.1 0.2 reduce_window_sum.11
  6.3 0.2 select_reduce_fusion.3
  6.5 0.8 broadcast_in_dim.201
  7.3 2.6 fusion.22
  9.9 0.1 select_reduce_fusion.2
  10.1 0.1 reshape.798
  10.2 0.1 reshape.799
  10.4 0.2 fusion.13
  10.6 0.6 fusion.9
  11.2 0.2 and_reduce_fusion
  11.7 0.8 convolution_convert_fusion
  12.5 1.4 copy.62
  13.8 1.7 pad_maximum_fusion
  15.5 15.4 %all-to-all-start = ((bf16[128,65,128]{2,1,0:T(8,128)(2,1)}), bf16[128,65,128]{2,1,0:T(8,128)(2,1)S(1)}, u32[]{:S(2)}, u32[]{:S(2)}) async-start(bf16[128,65,128]{2,1,0:T(8,128)(2,1)} %pad_maximum_fusion), calls=%async_computation | async-start | bytes 4718592 | tf_op jit(solution)/shard_map/all_to_all | solution.py:174
  31.0 13.1 %copy.63 = bf16[128,180,128]{1,2,0:T(8,128)(2,1)} copy(bf16[128,180,128]{2,0,1:T(8,128)(2,1)} %param.10) | data formatting | bytes 11796480 | tf_op args[2]
  44.0 9.1 %copy.64.p_ref = bf16[128,180,128]{2,1,0:T(8,128)(2,1)} copy(bf16[128,180,128]{2,0,1:T(8,128)(2,1)} %param.10) | data formatting | bytes 11796480 | tf_op args[2]
  53.1 35.9 %all-to-all-done = bf16[128,65,128]{2,1,0:T(8,128)(2,1)S(1)} async-done(((bf16[128,65,128]{2,1,0:T(8,128)(2,1)}), bf16[128,65,128]{2,1,0:T(8,128)(2,1)S(1)}, u32[]{:S(2)}, u32[]{:S(2)}) %all-to-all-start) | async-done | bytes 2129952 | tf_op jit(solution)/shard_map/all_to_all | solution.py:174
  89.1 0.5 fusion.11
  89.6 0.7 reshape.807.slot_ref
  90.3 0.7 reshape.808.qlen_ref
  91.0 1.6 slice.155
  92.7 47.7 %shard_map.103 = (bf16[256,32,128]{2,1,0:T(8,128)(2,1)}, f32[256,128]{1,0:T(8,128)}) custom-call(s32[256]{0:T(256)} %reshape.807.slot_ref, s32[256]{0:T(256)} %reshape.808.qlen_ref, s32[128]{0:T(128)} %len_ref.1, bf16[256,32,128]{2,1,0:T(8,128)(2,1)} %bitcast.46, bf16[128,180,128]{2,1,0:T(8,128)(2,1)} %copy.64.p_ref, bf16[128,128,180]{2,1,0:T(8,128)(2,1)} %bitcast.45), custom_call_target="tpu_custom_call" | custom-call | flops 754974720 | bytes 15990784 | tf_op jit(solution)/shard_map/pallas_call | solution.py:126
  140.4 1.0 slice_reduce_fusion
  141.4 0.1 squeeze.45
  141.6 0.2 slice_reduce_fusion.1
  141.8 0.2 slice_reduce_fusion.6
  142.0 0.2 slice_reduce_fusion.4
  142.1 1.1 fusion.10
  143.2 3.3 %pad_maximum_fusion.1 = bf16[128,65,128]{2,1,0:T(8,128)(2,1)} fusion(bf16[128,1,128]{2,1,0:T(2,128)(2,1)S(1)} %fusion.10, bf16[128,64,128]{2,1,0:T(8,128)(2,1)} %bitcast.48), kind=kLoop, calls=%fused_computation.1 | loop fusion | flops 4259840 | bytes 4259840 | tf_op jit(solution)/shard_map/concatenate | solution.py:181
  146.5 8.1 %all-to-all-start.1 = ((bf16[128,65,128]{2,1,0:T(8,128)(2,1)}), bf16[128,65,128]{2,1,0:T(8,128)(2,1)S(1)}, u32[]{:S(2)}, u32[]{:S(2)}) async-start(bf16[128,65,128]{2,1,0:T(8,128)(2,1)} %pad_maximum_fusion.1), calls=%async_computation.1 | async-start | bytes 4718592 | tf_op jit(solution)/shard_map/all_to_all | solution.py:184
  154.8 0.6 dynamic-slice
  156.1 0.2 dynamic-update-slice.1
  156.4 56.2 %all-to-all-done.1 = bf16[128,65,128]{2,1,0:T(8,128)(2,1)S(1)} async-done(((bf16[128,65,128]{2,1,0:T(8,128)(2,1)}), bf16[128,65,128]{2,1,0:T(8,128)(2,1)S(1)}, u32[]{:S(2)}, u32[]{:S(2)}) %all-to-all-start.1) | async-done | bytes 2129952 | tf_op jit(solution)/shard_map/all_to_all | solution.py:184
  212.7 0.2 copy.66
  212.9 0.2 reshape.809
  213.1 0.2 select_reduce_fusion
  213.4 0.1 reduce_max.19
  213.5 0.2 multiply_reduce_fusion.3
  213.7 0.2 dynamic-update-slice.3
  214.0 0.2 dynamic-update-slice
  214.2 0.2 dynamic-update-slice.2
  214.4 0.2 dynamic-update-slice.4
  214.6 2.7 %all-reduce.5 = (f32[8]{0:T(128)S(1)}, f32[8]{0:T(128)S(1)}, f32[8]{0:T(128)S(1)}, f32[8]{0:T(128)S(1)}, f32[8]{0:T(128)S(1)}) all-reduce(f32[8]{0:T(128)S(1)} %dynamic-update-slice.4, f32[8]{0:T(128)S(1)} %dynamic-update-slice.3, f32[8]{0:T(128)S(1)} %dynamic-update-slice.2, ...), channel_id=6, replica_groups=mesh['section'=2,'shard'=128] {'section'}, use_global_device_ids=true, to_apply=%add.4 | all-reduce | flops 40 | bytes 320
  217.2 0.6 subtract_add_fusion
  217.9 0.3 slice.163
  218.2 0.9 multiply_reduce_fusion
  219.3 0.3 collective-permute-start.1
  219.5 1.1 collective-permute-done.1
  220.6 0.2 multiply_reduce_fusion.1
  220.8 0.1 subtract_convert_fusion
  220.9 0.2 convolution_bitcast_fusion
  221.1 0.1 copy.68
  221.3 21.8 %all_to_all.20 = f32[128,3,128]{2,1,0:T(4,128)S(1)} all-to-all(f32[128,3,128]{2,1,0:T(4,128)S(1)} %reshape.805), channel_id=1, replica_groups=mesh['section'=2,'shard'=128] {'shard'}, dimensions={0} | all-to-all | bytes 393216 | tf_op jit(solution)/shard_map/all_to_all | solution.py:58
  243.2 0.1 reduce_sum.112
  243.3 0.7 broadcast_in_dim.220
  244.0 6.6 %all-to-all-start.3 = ((f32[128,3,128]{2,1,0:T(4,128)}), f32[128,3,128]{2,1,0:T(4,128)S(1)}, u32[]{:S(2)}, u32[]{:S(2)}) async-start(f32[128,3,128]{2,1,0:T(4,128)} %broadcast_in_dim.220), calls=%async_computation.3 | async-start | bytes 524288 | tf_op jit(solution)/shard_map/all_to_all | solution.py:60
  250.7 0.8 convolution_convert_fusion.1
  251.5 12.5 %all-to-all-done.3 = f32[128,3,128]{2,1,0:T(4,128)S(1)} async-done(((f32[128,3,128]{2,1,0:T(4,128)}), f32[128,3,128]{2,1,0:T(4,128)S(1)}, u32[]{:S(2)}, u32[]{:S(2)}) %all-to-all-start.3) | async-done | bytes 196640 | tf_op jit(solution)/shard_map/all_to_all | solution.py:60
  264.0 0.8 reshape.806
  (41 shorter events, 1.3 us)
Async XLA Ops:
  0.6 0.9 copy-start
  2.6 8.9 %collective-permute-start = (f32[4,32,128]{2,1,0:T(8,128)S(1)}, f32[4,32,128]{2,1,0:T(8,128)S(1)}, u32[]{:S(2)}, u32[]{:S(2)}) collective-permute-start(f32[4,32,128]{2,1,0:T(8,128)S(1)} %fusion.7), channel_id=1, source_target_pairs={{0,128},{128,0},{1,129},{129,1},{2,130},{130,2},{3,131},{131,3},{4... | collective-permute-start | bytes 196616 | tf_op jit(solution)/shard_map/ppermute | solution.py:53
  15.5 73.6 %all-to-all-start = ((bf16[128,65,128]{2,1,0:T(8,128)(2,1)}), bf16[128,65,128]{2,1,0:T(8,128)(2,1)S(1)}, u32[]{:S(2)}, u32[]{:S(2)}) async-start(bf16[128,65,128]{2,1,0:T(8,128)(2,1)} %pad_maximum_fusion), calls=%async_computation | async-start | bytes 4718592 | tf_op jit(solution)/shard_map/all_to_all | solution.py:174
  146.5 8.2 %copy-start.2 = (f32[4,32]{1,0:T(4,128)S(1)}, f32[4,32]{1,0:T(4,128)}, u32[]{:S(2)}) copy-start(f32[4,32]{1,0:T(4,128)} %param.15) | copy-start | bytes 1540
  146.5 8.3 %copy-start.4 = (u32[256]{0:T(256)S(1)}, u32[256]{0:T(256)}, u32[]{:S(2)}) copy-start(u32[256]{0:T(256)} %constant.67) | copy-start | bytes 3076
  146.5 9.8 %copy-start.3 = (s32[4]{0:T(128)S(1)}, s32[4]{0:T(128)}, u32[]{:S(2)}) copy-start(s32[4]{0:T(128)} %param.12) | copy-start | bytes 52
  146.5 66.1 %all-to-all-start.1 = ((bf16[128,65,128]{2,1,0:T(8,128)(2,1)}), bf16[128,65,128]{2,1,0:T(8,128)(2,1)S(1)}, u32[]{:S(2)}, u32[]{:S(2)}) async-start(bf16[128,65,128]{2,1,0:T(8,128)(2,1)} %pad_maximum_fusion.1), calls=%async_computation.1 | async-start | bytes 4718592 | tf_op jit(solution)/shard_map/all_to_all | solution.py:184
  219.2 31.5 %copy-start.1 = (bf16[384,128]{1,0:T(8,128)(2,1)S(1)}, bf16[384,128]{1,0:T(8,128)(2,1)}, u32[]{:S(2)}) copy-start(bf16[384,128]{1,0:T(8,128)(2,1)} %param.9) | copy-start | bytes 294916
  219.3 1.3 collective-permute-start.1
  244.0 19.9 %all-to-all-start.3 = ((f32[128,3,128]{2,1,0:T(4,128)}), f32[128,3,128]{2,1,0:T(4,128)S(1)}, u32[]{:S(2)}, u32[]{:S(2)}) async-start(f32[128,3,128]{2,1,0:T(4,128)} %broadcast_in_dim.220), calls=%async_computation.3 | async-start | bytes 524288 | tf_op jit(solution)/shard_map/all_to_all | solution.py:60
where the time goes:
time: 266 us; the launch traced here: 265 us
  waiting for transfers between devices  106 us (40%)
  Pallas kernels  47.7 us (18%)
  local copies, waits for them, and re-layouts  36.6 us (14%)
  starting transfers between devices  30.5 us (11%)
  blocking collectives  24.5 us (9%)
  other arithmetic  14.3 us (5%)
  matrix products  3.79 us (1%)
    all_to_all x1, waiting for transfers between devices, local(): got = lax.all_to_all(back, 'shard', 0, 0, tiled=True)  56.2 us
    pallas_call x1, Pallas kernels, owner_scores(): pl.pallas_call(score_kernel, grid_spec=grid_spec, out_shape=[jax.ShapeDty...  47.7 us
    all_to_all x1, waiting for transfers between devices, local(): recv = lax.all_to_all(payload, 'shard', 0, 0, tiled=True)  35.9 us
    unnamed x25, local copies, waits for them, and re-layouts  25.3 us
    all_to_all x1, blocking collectives, spread_sum(): summed = lax.all_to_all(pieces, axis, 0, 0, tiled=True).sum(axis=0)  21.8 us
    all_to_all x1, starting transfers between devices, local(): recv = lax.all_to_all(payload, 'shard', 0, 0, tiled=True)  15.4 us
    all_to_all x1, waiting for transfers between devices, spread_sum(): return lax.all_to_all(spread, axis, 0, 0, tiled=True).reshape(value.shape)  12.5 us
    all_to_all x1, starting transfers between devices, local(): got = lax.all_to_all(back, 'shard', 0, 0, tiled=True)  8.11 us
  transfers between devices with their start and end apart: 5, of which 4 were waited for; matrix products, arithmetic and copies ran while one was open for 12% of the time, Pallas kernels for 0%

commit v1 on v0

--- a/solution.py
+++ b/solution.py
@@ -78,30 +78,42 @@
 
 
 def score_kernel(slot_ref, qlen_ref, len_ref, q_ref, p_ref, pt_ref, pulled_ref, stud_ref):
-    group, num_tokens, _ = q_ref.shape
+    group, num_tokens, vec_dim = q_ref.shape
     pass_tokens = p_ref.shape[1]
     base = pl.program_id(0) * group
     for spot in range(group):
-        slot = slot_ref[base + spot]
-        limit = len_ref[slot]
-        logits = (
-            lax.dot_general(
-                p_ref[slot], q_ref[spot], (((1,), (1,)), ((), ())), preferred_element_type=jnp.float32
+        used = qlen_ref[base + spot] > 0
+
+        @pl.when(used)
+        def _score(spot=spot):
+            slot = slot_ref[base + spot]
+            limit = len_ref[slot]
+            logits = (
+                lax.dot_general(
+                    p_ref[slot],
+                    q_ref[spot],
+                    (((1,), (1,)), ((), ())),
+                    preferred_element_type=jnp.float32,
+                )
+                * SHARPNESS
             )
-            * SHARPNESS
-        )
-        in_range = lax.broadcasted_iota(jnp.int32, (pass_tokens, num_tokens), 0) < limit
-        logits = jnp.where(in_range, logits, NEGATIVE)
-        top_logit = jnp.max(logits, axis=0, keepdims=True)
-        expo_terms = jnp.where(in_range, jnp.exp(logits - top_logit), 0.0)
-        total = jnp.sum(expo_terms, axis=0, keepdims=True)
-        token_max = (top_logit + jnp.log(total)) / SHARPNESS
-        weight = (expo_terms / total).astype(jnp.bfloat16)
-        pulled = jnp.dot(pt_ref[slot], weight, preferred_element_type=jnp.float32)
-        pulled_ref[spot] = pulled.T.astype(jnp.bfloat16)
-        cols = lax.broadcasted_iota(jnp.int32, (1, num_tokens), 1)
-        score = jnp.sum(jnp.where(cols < qlen_ref[base + spot], token_max, 0.0))
-        stud_ref[pl.ds(spot, 1), :] = jnp.full((1, stud_ref.shape[1]), score, jnp.float32)
+            in_range = lax.broadcasted_iota(jnp.int32, (pass_tokens, num_tokens), 0) < limit
+            logits = jnp.where(in_range, logits, NEGATIVE)
+            top_logit = jnp.max(logits, axis=0, keepdims=True)
+            expo_terms = jnp.where(in_range, jnp.exp(logits - top_logit), 0.0)
+            total = jnp.sum(expo_terms, axis=0, keepdims=True)
+            token_max = (top_logit + jnp.log(total)) / SHARPNESS
+            weight = (expo_terms / total).astype(jnp.bfloat16)
+            pulled = jnp.dot(pt_ref[slot], weight, preferred_element_type=jnp.float32)
+            pulled_ref[spot] = pulled.T.astype(jnp.bfloat16)
+            cols = lax.broadcasted_iota(jnp.int32, (1, num_tokens), 1)
+            score = jnp.sum(jnp.where(cols < qlen_ref[base + spot], token_max, 0.0))
+            stud_ref[pl.ds(spot, 1), :] = jnp.full((1, stud_ref.shape[1]), score, jnp.float32)
+
+        @pl.when(jnp.logical_not(used))
+        def _empty(spot=spot):
+            pulled_ref[spot] = jnp.zeros((num_tokens, vec_dim), jnp.bfloat16)
+            stud_ref[pl.ds(spot, 1), :] = jnp.zeros((1, stud_ref.shape[1]), jnp.float32)
 
 
 def owner_scores(q_rows, passages, slot_at, qlen_at, pass_len):

time: 266 us -> 334 us (1.26)
  starting transfers between devices: 30.5 us -> 92.3 us
  Pallas kernels: 47.7 us -> 53.7 us
    all_to_all x1, starting transfers between devices: 8.11 us -> 69.9 us  [local(): got = lax.all_to_all(back, 'shard', 0, 0, tiled=True)]
    pallas_call x1, Pallas kernels: 47.7 us -> 53.7 us  [owner_scores(): pl.pallas_call(score_kernel, grid_spec=grid_spec, out_shape=[jax.ShapeDty...]
  transfers between devices with their start and end apart: 5 -> 5, of which waited for: 4 -> 4; matrix products, arithmetic and copies ran while one was open for 12% -> 10% of each run, Pallas kernels for 0% -> 0%
where the time goes in v1:
time: 334 us; the launch traced here: 332 us
  waiting for transfers between devices  106 us (32%)
  starting transfers between devices  92.3 us (28%)
  Pallas kernels  53.7 us (16%)
  local copies, waits for them, and re-layouts  36.6 us (11%)
  blocking collectives  24.6 us (7%)
  other arithmetic  14.3 us (4%)
  matrix products  3.79 us (1%)
    all_to_all x1, starting transfers between devices, local(): got = lax.all_to_all(back, 'shard', 0, 0, tiled=True)  69.9 us
    all_to_all x1, waiting for transfers between devices, local(): got = lax.all_to_all(back, 'shard', 0, 0, tiled=True)  56 us
    pallas_call x1, Pallas kernels, owner_scores(): pl.pallas_call(score_kernel, grid_spec=grid_spec, out_shape=[jax.ShapeDty...  53.7 us
    all_to_all x1, waiting for transfers between devices, local(): recv = lax.all_to_all(payload, 'shard', 0, 0, tiled=True)  35.9 us
    unnamed x25, local copies, waits for them, and re-layouts  25.3 us
    all_to_all x1, blocking collectives, spread_sum(): summed = lax.all_to_all(pieces, axis, 0, 0, tiled=True).sum(axis=0)  21.9 us
    all_to_all x1, starting transfers between devices, local(): recv = lax.all_to_all(payload, 'shard', 0, 0, tiled=True)  15.4 us
    all_to_all x1, waiting for transfers between devices, spread_sum(): return lax.all_to_all(spread, axis, 0, 0, tiled=True).reshape(value.shape)  12.5 us
  transfers between devices with their start and end apart: 5, of which 4 were waited for; matrix products, arithmetic and copies ran while one was open for 10% of the time, Pallas kernels for 0%

profile of v1, /device:TPU:2, one launch (start us, length us, event | category | flops | bytes accessed | tf_op | source)
XLA Modules:
  0.0 332.4 jit_solution(11716433174080327501)
XLA Ops:
  0.6 0.9 copy-done
  1.5 1.1 fusion.7
  2.7 1.5 fusion.28
  4.2 0.5 broadcast.645
  4.7 1.3 broadcast_multiply_fusion
  6.1 0.2 reduce_window_sum.11
  6.3 0.2 select_reduce_fusion.3
  6.5 0.8 broadcast_in_dim.201
  7.3 2.6 fusion.22
  9.9 0.1 select_reduce_fusion.2
  10.1 0.1 reshape.798
  10.2 0.1 reshape.799
  10.4 0.2 fusion.13
  10.6 0.6 fusion.9
  11.2 0.2 and_reduce_fusion
  11.7 0.8 convolution_convert_fusion
  12.5 1.4 copy.62
  13.8 1.7 pad_maximum_fusion
  15.5 15.4 %all-to-all-start = ((bf16[128,65,128]{2,1,0:T(8,128)(2,1)}), bf16[128,65,128]{2,1,0:T(8,128)(2,1)S(1)}, u32[]{:S(2)}, u32[]{:S(2)}) async-start(bf16[128,65,128]{2,1,0:T(8,128)(2,1)} %pad_maximum_fusion), calls=%async_computation | async-start | bytes 4718592 | tf_op jit(solution)/shard_map/all_to_all | solution.py:186
  31.0 13.1 %copy.63 = bf16[128,180,128]{1,2,0:T(8,128)(2,1)} copy(bf16[128,180,128]{2,0,1:T(8,128)(2,1)} %param.10) | data formatting | bytes 11796480 | tf_op args[2]
  44.0 9.1 %copy.64.p_ref = bf16[128,180,128]{2,1,0:T(8,128)(2,1)} copy(bf16[128,180,128]{2,0,1:T(8,128)(2,1)} %param.10) | data formatting | bytes 11796480 | tf_op args[2]
  53.1 35.9 %all-to-all-done = bf16[128,65,128]{2,1,0:T(8,128)(2,1)S(1)} async-done(((bf16[128,65,128]{2,1,0:T(8,128)(2,1)}), bf16[128,65,128]{2,1,0:T(8,128)(2,1)S(1)}, u32[]{:S(2)}, u32[]{:S(2)}) %all-to-all-start) | async-done | bytes 2129952 | tf_op jit(solution)/shard_map/all_to_all | solution.py:186
  89.1 0.5 fusion.11
  89.6 0.7 reshape.807.slot_ref
  90.3 0.7 reshape.808.qlen_ref
  91.0 1.6 slice.155
  92.7 53.7 %shard_map.103 = (bf16[256,32,128]{2,1,0:T(8,128)(2,1)}, f32[256,128]{1,0:T(8,128)}) custom-call(s32[256]{0:T(256)} %reshape.807.slot_ref, s32[256]{0:T(256)} %reshape.808.qlen_ref, s32[128]{0:T(128)} %len_ref.1, bf16[256,32,128]{2,1,0:T(8,128)(2,1)} %bitcast.46, bf16[128,180,128]{2,1,0:T(8,128)(2,1)} %copy.64.p_ref, bf16[128,128,180]{2,1,0:T(8,128)(2,1)} %bitcast.45), custom_call_target="tpu_custom_call" | custom-call | flops 754974720 | bytes 15990784 | tf_op jit(solution)/shard_map/pallas_call | solution.py:138
  146.4 1.0 slice_reduce_fusion
  147.4 0.1 squeeze.45
  147.6 0.2 slice_reduce_fusion.1
  147.7 0.2 slice_reduce_fusion.6
  147.9 0.2 slice_reduce_fusion.4
  148.1 1.1 fusion.10
  149.2 3.3 pad_maximum_fusion.1
  152.5 69.9 %all-to-all-start.1 = ((bf16[128,65,128]{2,1,0:T(8,128)(2,1)}), bf16[128,65,128]{2,1,0:T(8,128)(2,1)S(1)}, u32[]{:S(2)}, u32[]{:S(2)}) async-start(bf16[128,65,128]{2,1,0:T(8,128)(2,1)} %pad_maximum_fusion.1), calls=%async_computation.1 | async-start | bytes 4718592 | tf_op jit(solution)/shard_map/all_to_all | solution.py:196
  222.6 0.6 dynamic-slice
  223.9 0.2 dynamic-update-slice.1
  224.2 56.0 %all-to-all-done.1 = bf16[128,65,128]{2,1,0:T(8,128)(2,1)S(1)} async-done(((bf16[128,65,128]{2,1,0:T(8,128)(2,1)}), bf16[128,65,128]{2,1,0:T(8,128)(2,1)S(1)}, u32[]{:S(2)}, u32[]{:S(2)}) %all-to-all-start.1) | async-done | bytes 2129952 | tf_op jit(solution)/shard_map/all_to_all | solution.py:196
  280.3 0.2 copy.66
  280.5 0.2 reshape.809
  280.6 0.2 select_reduce_fusion
  280.9 0.1 reduce_max.19
  281.0 0.2 multiply_reduce_fusion.3
  281.3 0.2 dynamic-update-slice.3
  281.5 0.2 dynamic-update-slice
  281.7 0.2 dynamic-update-slice.2
  281.9 0.2 dynamic-update-slice.4
  282.1 2.7 all-reduce.5
  284.8 0.6 subtract_add_fusion
  285.5 0.3 slice.163
  285.8 0.9 multiply_reduce_fusion
  286.8 0.3 collective-permute-start.1
  287.1 1.1 collective-permute-done.1
  288.1 0.2 multiply_reduce_fusion.1
  288.3 0.1 subtract_convert_fusion
  288.5 0.2 convolution_bitcast_fusion
  288.7 0.1 copy.68
  288.9 21.9 %all_to_all.20 = f32[128,3,128]{2,1,0:T(4,128)S(1)} all-to-all(f32[128,3,128]{2,1,0:T(4,128)S(1)} %reshape.805), channel_id=1, replica_groups=mesh['section'=2,'shard'=128] {'shard'}, dimensions={0} | all-to-all | bytes 393216 | tf_op jit(solution)/shard_map/all_to_all | solution.py:58
  310.8 0.1 reduce_sum.112
  310.9 0.7 broadcast_in_dim.220
  311.7 6.6 %all-to-all-start.3 = ((f32[128,3,128]{2,1,0:T(4,128)}), f32[128,3,128]{2,1,0:T(4,128)S(1)}, u32[]{:S(2)}, u32[]{:S(2)}) async-start(f32[128,3,128]{2,1,0:T(4,128)} %broadcast_in_dim.220), calls=%async_computation.3 | async-start | bytes 524288 | tf_op jit(solution)/shard_map/all_to_all | solution.py:60
  318.3 0.8 convolution_convert_fusion.1
  319.1 12.5 %all-to-all-done.3 = f32[128,3,128]{2,1,0:T(4,128)S(1)} async-done(((f32[128,3,128]{2,1,0:T(4,128)}), f32[128,3,128]{2,1,0:T(4,128)S(1)}, u32[]{:S(2)}, u32[]{:S(2)}) %all-to-all-start.3) | async-done | bytes 196640 | tf_op jit(solution)/shard_map/all_to_all | solution.py:60
  331.6 0.8 reshape.806
  (41 shorter events, 1.3 us)
Async XLA Ops:
  0.6 0.9 copy-start
  2.6 8.9 %collective-permute-start = (f32[4,32,128]{2,1,0:T(8,128)S(1)}, f32[4,32,128]{2,1,0:T(8,128)S(1)}, u32[]{:S(2)}, u32[]{:S(2)}) collective-permute-start(f32[4,32,128]{2,1,0:T(8,128)S(1)} %fusion.7), channel_id=1, source_target_pairs={{0,128},{128,0},{1,129},{129,1},{2,130},{130,2},{3,131},{131,3},{4... | collective-permute-start | bytes 196616 | tf_op jit(solution)/shard_map/ppermute | solution.py:53
  15.5 73.6 %all-to-all-start = ((bf16[128,65,128]{2,1,0:T(8,128)(2,1)}), bf16[128,65,128]{2,1,0:T(8,128)(2,1)S(1)}, u32[]{:S(2)}, u32[]{:S(2)}) async-start(bf16[128,65,128]{2,1,0:T(8,128)(2,1)} %pad_maximum_fusion), calls=%async_computation | async-start | bytes 4718592 | tf_op jit(solution)/shard_map/all_to_all | solution.py:186
  152.5 70.0 %copy-start.2 = (f32[4,32]{1,0:T(4,128)S(1)}, f32[4,32]{1,0:T(4,128)}, u32[]{:S(2)}) copy-start(f32[4,32]{1,0:T(4,128)} %param.15) | copy-start | bytes 1540
  152.5 70.1 %copy-start.4 = (u32[256]{0:T(256)S(1)}, u32[256]{0:T(256)}, u32[]{:S(2)}) copy-start(u32[256]{0:T(256)} %constant.67) | copy-start | bytes 3076
  152.5 71.6 %copy-start.3 = (s32[4]{0:T(128)S(1)}, s32[4]{0:T(128)}, u32[]{:S(2)}) copy-start(s32[4]{0:T(128)} %param.12) | copy-start | bytes 52
  152.5 127.7 %all-to-all-start.1 = ((bf16[128,65,128]{2,1,0:T(8,128)(2,1)}), bf16[128,65,128]{2,1,0:T(8,128)(2,1)S(1)}, u32[]{:S(2)}, u32[]{:S(2)}) async-start(bf16[128,65,128]{2,1,0:T(8,128)(2,1)} %pad_maximum_fusion.1), calls=%async_computation.1 | async-start | bytes 4718592 | tf_op jit(solution)/shard_map/all_to_all | solution.py:196
  286.7 31.6 %copy-start.1 = (bf16[384,128]{1,0:T(8,128)(2,1)S(1)}, bf16[384,128]{1,0:T(8,128)(2,1)}, u32[]{:S(2)}) copy-start(bf16[384,128]{1,0:T(8,128)(2,1)} %param.9) | copy-start | bytes 294916
  286.8 1.3 collective-permute-start.1
  311.7 19.9 %all-to-all-start.3 = ((f32[128,3,128]{2,1,0:T(4,128)}), f32[128,3,128]{2,1,0:T(4,128)S(1)}, u32[]{:S(2)}, u32[]{:S(2)}) async-start(f32[128,3,128]{2,1,0:T(4,128)} %broadcast_in_dim.220), calls=%async_computation.3 | async-start | bytes 524288 | tf_op jit(solution)/shard_map/all_to_all | solution.py:60

commit v2 on v1

--- a/solution.py
+++ b/solution.py
@@ -9,7 +9,7 @@
 EPSILON = 1e-06
 NEGATIVE = -1e30
 CAPACITY = 2
-GROUP = 8
+GROUP = 16
 
 
 def combined_all(value, axis, join):
@@ -77,23 +77,23 @@
     return row.astype(jnp.bfloat16)[:, None, :]
 
 
-def score_kernel(slot_ref, qlen_ref, len_ref, q_ref, p_ref, pt_ref, pulled_ref, stud_ref):
-    group, num_tokens, vec_dim = q_ref.shape
+def score_kernel(
+    count_ref, order_ref, slot_ref, qlen_ref, len_ref, q_ref, p_ref, pt_ref, pulled_ref, stud_ref
+):
+    _, num_tokens, vec_dim = q_ref.shape
     pass_tokens = p_ref.shape[1]
+    group = GROUP
     base = pl.program_id(0) * group
-    for spot in range(group):
-        used = qlen_ref[base + spot] > 0
-
-        @pl.when(used)
-        def _score(spot=spot):
-            slot = slot_ref[base + spot]
+
+    @pl.when(base < count_ref[0])
+    def _score():
+        for spot in range(group):
+            at = order_ref[base + spot]
+            slot = slot_ref[at]
             limit = len_ref[slot]
             logits = (
                 lax.dot_general(
-                    p_ref[slot],
-                    q_ref[spot],
-                    (((1,), (1,)), ((), ())),
-                    preferred_element_type=jnp.float32,
+                    p_ref[slot], q_ref[at], (((1,), (1,)), ((), ())), preferred_element_type=jnp.float32
                 )
                 * SHARPNESS
             )
@@ -105,32 +105,42 @@
             token_max = (top_logit + jnp.log(total)) / SHARPNESS
             weight = (expo_terms / total).astype(jnp.bfloat16)
             pulled = jnp.dot(pt_ref[slot], weight, preferred_element_type=jnp.float32)
-            pulled_ref[spot] = pulled.T.astype(jnp.bfloat16)
+            pulled_ref[at] = pulled.T.astype(jnp.bfloat16)
             cols = lax.broadcasted_iota(jnp.int32, (1, num_tokens), 1)
-            score = jnp.sum(jnp.where(cols < qlen_ref[base + spot], token_max, 0.0))
-            stud_ref[pl.ds(spot, 1), :] = jnp.full((1, stud_ref.shape[1]), score, jnp.float32)
-
-        @pl.when(jnp.logical_not(used))
-        def _empty(spot=spot):
-            pulled_ref[spot] = jnp.zeros((num_tokens, vec_dim), jnp.bfloat16)
-            stud_ref[pl.ds(spot, 1), :] = jnp.zeros((1, stud_ref.shape[1]), jnp.float32)
+            score = jnp.sum(jnp.where(cols < qlen_ref[at], token_max, 0.0))
+            stud_ref[pl.ds(at, 1), :] = jnp.full((1, stud_ref.shape[1]), score, jnp.float32)
+
+    @pl.when(base >= count_ref[0])
+    def _empty():
+        for spot in range(group):
+            at = order_ref[base + spot]
+            pulled_ref[at] = jnp.zeros((num_tokens, vec_dim), jnp.bfloat16)
+            stud_ref[pl.ds(at, 1), :] = jnp.zeros((1, stud_ref.shape[1]), jnp.float32)
 
 
 def owner_scores(q_rows, passages, slot_at, qlen_at, pass_len):
     slots, num_tokens, vec_dim = q_rows.shape
     held, pass_tokens, _ = passages.shape
-    group = GROUP
+    used = qlen_at > 0
+    count = jnp.sum(used.astype(jnp.int32))
+    place = jnp.where(
+        used, jnp.cumsum(used) - 1, count + jnp.cumsum(jnp.logical_not(used)) - 1
+    ).astype(jnp.int32)
+    order = jnp.sum(
+        jnp.where(place[None, :] == jnp.arange(slots)[:, None], jnp.arange(slots)[None, :], 0), axis=1
+    ).astype(jnp.int32)
+    whole = lambda i, *_: (0, 0, 0)
     grid_spec = pltpu.PrefetchScalarGridSpec(
-        num_scalar_prefetch=3,
-        grid=(slots // group,),
+        num_scalar_prefetch=5,
+        grid=(slots // GROUP,),
         in_specs=[
-            pl.BlockSpec((group, num_tokens, vec_dim), lambda i, *_: (i, 0, 0)),
-            pl.BlockSpec((held, pass_tokens, vec_dim), lambda i, *_: (0, 0, 0)),
-            pl.BlockSpec((held, vec_dim, pass_tokens), lambda i, *_: (0, 0, 0)),
+            pl.BlockSpec((slots, num_tokens, vec_dim), whole),
+            pl.BlockSpec((held, pass_tokens, vec_dim), whole),
+            pl.BlockSpec((held, vec_dim, pass_tokens), whole),
         ],
         out_specs=[
-            pl.BlockSpec((group, num_tokens, vec_dim), lambda i, *_: (i, 0, 0)),
-            pl.BlockSpec((group, 128), lambda i, *_: (i, 0)),
+            pl.BlockSpec((slots, num_tokens, vec_dim), whole),
+            pl.BlockSpec((slots, 128), lambda i, *_: (0, 0)),
         ],
     )
     flops = 4 * slots * num_tokens * pass_tokens * vec_dim
@@ -146,7 +156,16 @@
         cost_estimate=pl.CostEstimate(
             flops=flops, transcendentals=slots * num_tokens * pass_tokens, bytes_accessed=moved
         ),
-    )(slot_at, qlen_at, pass_len, q_rows, passages, jnp.swapaxes(passages, 1, 2))
+    )(
+        count.reshape(1),
+        order,
+        slot_at,
+        qlen_at,
+        pass_len,
+        q_rows,
+        passages,
+        jnp.swapaxes(passages, 1, 2),
+    )
 
 
 def local(hidden, proj, passages, pass_len, query_len, cand_owner, cand_slot, teacher):

time: 334 us -> 268 us (0.80)
  starting transfers between devices: 92.3 us -> 51.4 us
  Pallas kernels: 53.7 us -> 25.7 us
    all_to_all x1, starting transfers between devices: 69.9 us -> 29 us  [local(): got = lax.all_to_all(back, 'shard', 0, 0, tiled=True)]
    pallas_call x1, Pallas kernels: 53.7 us -> 25.7 us  [owner_scores(): pl.pallas_call(score_kernel, grid_spec=grid_spec, out_shape=[jax.ShapeDty...]
    unnamed x25 -> x27, local copies, waits for them, and re-layouts: 25.3 us -> 25.3 us
  transfers between devices with their start and end apart: 5 -> 5, of which waited for: 4 -> 4; matrix products, arithmetic and copies ran while one was open for 10% -> 12% of each run, Pallas kernels for 0% -> 0%
where the time goes in v2:
time: 268 us; the launch traced here: 267 us
  waiting for transfers between devices  106 us (40%)
  starting transfers between devices  51.4 us (19%)
  local copies, waits for them, and re-layouts  36.7 us (14%)
  Pallas kernels  25.7 us (10%)
  blocking collectives  24.4 us (9%)
  other arithmetic  17.3 us (6%)
  matrix products  3.78 us (1%)
    all_to_all x1, waiting for transfers between devices, local(): got = lax.all_to_all(back, 'shard', 0, 0, tiled=True)  56.3 us
    all_to_all x1, waiting for transfers between devices, local(): recv = lax.all_to_all(payload, 'shard', 0, 0, tiled=True)  35.9 us
    all_to_all x1, starting transfers between devices, local(): got = lax.all_to_all(back, 'shard', 0, 0, tiled=True)  29 us
    pallas_call x1, Pallas kernels, owner_scores(): pl.pallas_call(score_kernel, grid_spec=grid_spec, out_shape=[jax.ShapeDty...  25.7 us
    unnamed x27, local copies, waits for them, and re-layouts  25.3 us
    all_to_all x1, blocking collectives, spread_sum(): summed = lax.all_to_all(pieces, axis, 0, 0, tiled=True).sum(axis=0)  21.9 us
    all_to_all x1, starting transfers between devices, local(): recv = lax.all_to_all(payload, 'shard', 0, 0, tiled=True)  15.4 us
    all_to_all x1, waiting for transfers between devices, spread_sum(): return lax.all_to_all(spread, axis, 0, 0, tiled=True).reshape(value.shape)  12.5 us
  transfers between devices with their start and end apart: 5, of which 4 were waited for; matrix products, arithmetic and copies ran while one was open for 12% of the time, Pallas kernels for 0%

profile of v2, /device:TPU:2, one launch (start us, length us, event | category | flops | bytes accessed | tf_op | source)
XLA Modules:
  0.0 266.7 jit_solution(3224523748564952453)
XLA Ops:
  0.6 0.9 copy-done
  1.5 1.1 fusion.7
  2.7 1.5 fusion.31
  4.2 0.5 broadcast.699
  4.7 1.3 broadcast_multiply_fusion
  6.1 0.2 reduce_window_sum.40
  6.3 0.2 select_reduce_fusion.4
  6.5 0.8 broadcast_in_dim.216
  7.3 2.6 fusion.24
  9.9 0.1 select_reduce_fusion.3
  10.4 0.2 fusion.13
  10.6 0.6 fusion.9
  11.2 0.2 and_reduce_fusion
  11.7 0.8 convolution_convert_fusion
  12.5 1.4 copy.62
  13.8 1.7 pad_maximum_fusion
  15.5 15.4 %all-to-all-start = ((bf16[128,65,128]{2,1,0:T(8,128)(2,1)}), bf16[128,65,128]{2,1,0:T(8,128)(2,1)S(1)}, u32[]{:S(2)}, u32[]{:S(2)}) async-start(bf16[128,65,128]{2,1,0:T(8,128)(2,1)} %pad_maximum_fusion), calls=%async_computation | async-start | bytes 4718592 | tf_op jit(solution)/shard_map/all_to_all | solution.py:205
  31.0 13.1 %copy.63 = bf16[128,180,128]{1,2,0:T(8,128)(2,1)} copy(bf16[128,180,128]{2,0,1:T(8,128)(2,1)} %param.10) | data formatting | bytes 11796480 | tf_op args[2]
  44.0 9.1 %copy.64.p_ref = bf16[128,180,128]{2,1,0:T(8,128)(2,1)} copy(bf16[128,180,128]{2,0,1:T(8,128)(2,1)} %param.10) | data formatting | bytes 11796480 | tf_op args[2]
  53.1 35.9 %all-to-all-done = bf16[128,65,128]{2,1,0:T(8,128)(2,1)S(1)} async-done(((bf16[128,65,128]{2,1,0:T(8,128)(2,1)}), bf16[128,65,128]{2,1,0:T(8,128)(2,1)S(1)}, u32[]{:S(2)}, u32[]{:S(2)}) %all-to-all-start) | async-done | bytes 2129952 | tf_op jit(solution)/shard_map/all_to_all | solution.py:205
  89.1 1.4 fusion.12
  90.6 0.3 reduce-window.24
  91.2 0.1 reshape.884
  91.3 0.3 reduce-window.16
  91.9 0.1 reshape.883.qlen_ref
  92.0 0.7 compare_select_fusion.4
  92.7 0.7 select_reduce_fusion.1.order_ref
  93.4 0.7 reshape.886.slot_ref
  94.1 1.6 slice.173
  95.8 25.7 %shard_map.103 = (bf16[256,32,128]{2,1,0:T(8,128)(2,1)}, f32[256,128]{1,0:T(8,128)}) custom-call(s32[1]{0:T(128)} %bitcast.8.count_ref, s32[256]{0:T(256)} %select_reduce_fusion.1.order_ref, s32[256]{0:T(256)} %reshape.886.slot_ref, s32[256]{0:T(256)} %copy-done.3, s32[128]{0:T(128)} %len_ref.1, bf16[256,32,128]{2,1,0:T(8,128)(2,1)} %bitcast.51, ...), custom_call_target="tpu_custom_call" | custom-call | flops 754974720 | bytes 15990784 | tf_op jit(solution)/shard_map/pallas_call | solution.py:148
  121.5 1.0 slice_reduce_fusion
  122.5 0.1 squeeze.45
  122.7 0.2 slice_reduce_fusion.1
  122.8 0.2 slice_reduce_fusion.6
  123.0 0.2 slice_reduce_fusion.4
  123.2 1.1 fusion.10
  124.3 3.3 %pad_maximum_fusion.1 = bf16[128,65,128]{2,1,0:T(8,128)(2,1)} fusion(bf16[128,1,128]{2,1,0:T(2,128)(2,1)S(1)} %fusion.10, bf16[128,64,128]{2,1,0:T(8,128)(2,1)} %bitcast.53), kind=kLoop, calls=%fused_computation.1 | loop fusion | flops 4259840 | bytes 4259840 | tf_op jit(solution)/shard_map/concatenate | solution.py:212
  127.6 29.0 %all-to-all-start.1 = ((bf16[128,65,128]{2,1,0:T(8,128)(2,1)}), bf16[128,65,128]{2,1,0:T(8,128)(2,1)S(1)}, u32[]{:S(2)}, u32[]{:S(2)}) async-start(bf16[128,65,128]{2,1,0:T(8,128)(2,1)} %pad_maximum_fusion.1), calls=%async_computation.1 | async-start | bytes 4718592 | tf_op jit(solution)/shard_map/all_to_all | solution.py:215
  156.8 0.6 dynamic-slice
  158.1 0.2 dynamic-update-slice.1
  158.4 56.3 %all-to-all-done.1 = bf16[128,65,128]{2,1,0:T(8,128)(2,1)S(1)} async-done(((bf16[128,65,128]{2,1,0:T(8,128)(2,1)}), bf16[128,65,128]{2,1,0:T(8,128)(2,1)S(1)}, u32[]{:S(2)}, u32[]{:S(2)}) %all-to-all-start.1) | async-done | bytes 2129952 | tf_op jit(solution)/shard_map/all_to_all | solution.py:215
  214.8 0.2 copy.66
  215.0 0.2 reshape.887
  215.2 0.2 select_reduce_fusion
  215.6 0.2 multiply_reduce_fusion.3
  215.8 0.2 dynamic-update-slice.3
  216.1 0.2 dynamic-update-slice
  216.3 0.2 dynamic-update-slice.2
  216.5 0.2 dynamic-update-slice.4
  216.7 2.4 all-reduce.5
  219.1 0.6 subtract_add_fusion
  219.8 0.3 slice.181
  220.1 0.9 multiply_reduce_fusion
  221.1 0.3 collective-permute-start.1
  221.4 1.1 collective-permute-done.1
  222.5 0.2 multiply_reduce_fusion.1
  222.8 0.2 convolution_bitcast_fusion
  223.2 21.9 %all_to_all.20 = f32[128,3,128]{2,1,0:T(4,128)S(1)} all-to-all(f32[128,3,128]{2,1,0:T(4,128)S(1)} %reshape.881), channel_id=1, replica_groups=mesh['section'=2,'shard'=128] {'shard'}, dimensions={0} | all-to-all | bytes 393216 | tf_op jit(solution)/shard_map/all_to_all | solution.py:58
  245.2 0.1 reduce_sum.132
  245.3 0.7 broadcast_in_dim.237
  246.0 6.6 %all-to-all-start.3 = ((f32[128,3,128]{2,1,0:T(4,128)}), f32[128,3,128]{2,1,0:T(4,128)S(1)}, u32[]{:S(2)}, u32[]{:S(2)}) async-start(f32[128,3,128]{2,1,0:T(4,128)} %broadcast_in_dim.237), calls=%async_computation.3 | async-start | bytes 524288 | tf_op jit(solution)/shard_map/all_to_all | solution.py:60
  252.6 0.8 convolution_convert_fusion.1
  253.5 12.5 %all-to-all-done.3 = f32[128,3,128]{2,1,0:T(4,128)S(1)} async-done(((f32[128,3,128]{2,1,0:T(4,128)}), f32[128,3,128]{2,1,0:T(4,128)S(1)}, u32[]{:S(2)}, u32[]{:S(2)}) %all-to-all-start.3) | async-done | bytes 196640 | tf_op jit(solution)/shard_map/all_to_all | solution.py:60
  266.0 0.8 reshape.882
  (55 shorter events, 2.6 us)
Async XLA Ops:
  0.6 0.9 copy-start
  2.6 8.9 %collective-permute-start = (f32[4,32,128]{2,1,0:T(8,128)S(1)}, f32[4,32,128]{2,1,0:T(8,128)S(1)}, u32[]{:S(2)}, u32[]{:S(2)}) collective-permute-start(f32[4,32,128]{2,1,0:T(8,128)S(1)} %fusion.7), channel_id=1, source_target_pairs={{0,128},{128,0},{1,129},{129,1},{2,130},{130,2},{3,131},{131,3},{4... | collective-permute-start | bytes 196616 | tf_op jit(solution)/shard_map/ppermute | solution.py:53
  15.5 73.6 %all-to-all-start = ((bf16[128,65,128]{2,1,0:T(8,128)(2,1)}), bf16[128,65,128]{2,1,0:T(8,128)(2,1)S(1)}, u32[]{:S(2)}, u32[]{:S(2)}) async-start(bf16[128,65,128]{2,1,0:T(8,128)(2,1)} %pad_maximum_fusion), calls=%async_computation | async-start | bytes 4718592 | tf_op jit(solution)/shard_map/all_to_all | solution.py:205
  92.0 3.8 %copy-start.3 = (s32[256]{0:T(256)}, s32[256]{0:T(256)S(1)}, u32[]{:S(2)}) copy-start(s32[256]{0:T(256)S(1)} %reshape.883.qlen_ref) | copy-start | bytes 3076
  127.6 29.1 %copy-start.2 = (f32[4,32]{1,0:T(4,128)S(1)}, f32[4,32]{1,0:T(4,128)}, u32[]{:S(2)}) copy-start(f32[4,32]{1,0:T(4,128)} %param.15) | copy-start | bytes 1540
  127.6 29.3 %copy-start.5 = (u32[256]{0:T(256)S(1)}, u32[256]{0:T(256)}, u32[]{:S(2)}) copy-start(u32[256]{0:T(256)} %constant.75) | copy-start | bytes 3076
  127.6 30.8 %copy-start.4 = (s32[4]{0:T(128)S(1)}, s32[4]{0:T(128)}, u32[]{:S(2)}) copy-start(s32[4]{0:T(128)} %param.12) | copy-start | bytes 52
  127.6 87.1 %all-to-all-start.1 = ((bf16[128,65,128]{2,1,0:T(8,128)(2,1)}), bf16[128,65,128]{2,1,0:T(8,128)(2,1)S(1)}, u32[]{:S(2)}, u32[]{:S(2)}) async-start(bf16[128,65,128]{2,1,0:T(8,128)(2,1)} %pad_maximum_fusion.1), calls=%async_computation.1 | async-start | bytes 4718592 | tf_op jit(solution)/shard_map/all_to_all | solution.py:215
  221.0 31.6 %copy-start.1 = (bf16[384,128]{1,0:T(8,128)(2,1)S(1)}, bf16[384,128]{1,0:T(8,128)(2,1)}, u32[]{:S(2)}) copy-start(bf16[384,128]{1,0:T(8,128)(2,1)} %param.9) | copy-start | bytes 294916
  221.1 1.3 collective-permute-start.1
  246.0 19.9 %all-to-all-start.3 = ((f32[128,3,128]{2,1,0:T(4,128)}), f32[128,3,128]{2,1,0:T(4,128)S(1)}, u32[]{:S(2)}, u32[]{:S(2)}) async-start(f32[128,3,128]{2,1,0:T(4,128)} %broadcast_in_dim.237), calls=%async_computation.3 | async-start | bytes 524288 | tf_op jit(solution)/shard_map/all_to_all | solution.py:60

commit v3 on v0

--- a/solution.py
+++ b/solution.py
@@ -9,7 +9,7 @@
 EPSILON = 1e-06
 NEGATIVE = -1e30
 CAPACITY = 2
-GROUP = 8
+GROUP = 16
 
 
 def combined_all(value, axis, join):

time: 266 us -> 262 us (0.985)
  Pallas kernels: 47.7 us -> 44.6 us
    pallas_call x1, Pallas kernels: 47.7 us -> 44.6 us  [owner_scores(): pl.pallas_call(score_kernel, grid_spec=grid_spec, out_shape=[jax.ShapeDty...]
  transfers between devices with their start and end apart: 5 -> 5, of which waited for: 4 -> 4; matrix products, arithmetic and copies ran while one was open for 12% -> 13% of each run, Pallas kernels for 0% -> 0%
where the time goes in v3:
time: 262 us; the launch traced here: 261 us
  waiting for transfers between devices  106 us (40%)
  Pallas kernels  44.6 us (17%)
  local copies, waits for them, and re-layouts  36.6 us (14%)
  starting transfers between devices  30.5 us (12%)
  blocking collectives  24.3 us (9%)
  other arithmetic  14.3 us (5%)
  matrix products  3.79 us (1%)
    all_to_all x1, waiting for transfers between devices, local(): got = lax.all_to_all(back, 'shard', 0, 0, tiled=True)  56.2 us
    pallas_call x1, Pallas kernels, owner_scores(): pl.pallas_call(score_kernel, grid_spec=grid_spec, out_shape=[jax.ShapeDty...  44.6 us
    all_to_all x1, waiting for transfers between devices, local(): recv = lax.all_to_all(payload, 'shard', 0, 0, tiled=True)  35.9 us
    unnamed x25, local copies, waits for them, and re-layouts  25.3 us
    all_to_all x1, blocking collectives, spread_sum(): summed = lax.all_to_all(pieces, axis, 0, 0, tiled=True).sum(axis=0)  21.8 us
    all_to_all x1, starting transfers between devices, local(): recv = lax.all_to_all(payload, 'shard', 0, 0, tiled=True)  15.4 us
    all_to_all x1, waiting for transfers between devices, spread_sum(): return lax.all_to_all(spread, axis, 0, 0, tiled=True).reshape(value.shape)  12.5 us
    all_to_all x1, starting transfers between devices, local(): got = lax.all_to_all(back, 'shard', 0, 0, tiled=True)  8.16 us
  transfers between devices with their start and end apart: 5, of which 4 were waited for; matrix products, arithmetic and copies ran while one was open for 13% of the time, Pallas kernels for 0%

profile of v3, /device:TPU:2, one launch (start us, length us, event | category | flops | bytes accessed | tf_op | source)
XLA Modules:
  0.0 261.4 jit_solution(12498466219963797460)
XLA Ops:
  0.6 0.9 copy-done
  1.5 1.1 fusion.7
  2.7 1.5 fusion.28
  4.2 0.5 broadcast.645
  4.7 1.3 broadcast_multiply_fusion
  6.1 0.2 reduce_window_sum.11
  6.3 0.2 select_reduce_fusion.3
  6.5 0.8 broadcast_in_dim.201
  7.3 2.6 %fusion.22 = s32[128]{0:T(128)S(1)} fusion(s32[]{:T(128)} %bitcast.3, s32[]{:T(128)} %bitcast.4, s32[]{:T(128)} %bitcast.6, s32[]{:T(128)} %bitcast.5), kind=kLoop, calls=%fused_computation.84 | loop fusion | flops 2176 | bytes 528 | tf_op jit(solution)/shard_map/gather | solution.py:169
  9.9 0.1 select_reduce_fusion.2
  10.1 0.1 reshape.798
  10.2 0.1 reshape.799
  10.4 0.2 fusion.13
  10.6 0.6 fusion.9
  11.2 0.2 and_reduce_fusion
  11.7 0.8 convolution_convert_fusion
  12.5 1.4 copy.62
  13.8 1.7 pad_maximum_fusion
  15.5 15.4 %all-to-all-start = ((bf16[128,65,128]{2,1,0:T(8,128)(2,1)}), bf16[128,65,128]{2,1,0:T(8,128)(2,1)S(1)}, u32[]{:S(2)}, u32[]{:S(2)}) async-start(bf16[128,65,128]{2,1,0:T(8,128)(2,1)} %pad_maximum_fusion), calls=%async_computation | async-start | bytes 4718592 | tf_op jit(solution)/shard_map/all_to_all | solution.py:174
  31.0 13.1 %copy.63 = bf16[128,180,128]{1,2,0:T(8,128)(2,1)} copy(bf16[128,180,128]{2,0,1:T(8,128)(2,1)} %param.10) | data formatting | bytes 11796480 | tf_op args[2]
  44.0 9.1 %copy.64.p_ref = bf16[128,180,128]{2,1,0:T(8,128)(2,1)} copy(bf16[128,180,128]{2,0,1:T(8,128)(2,1)} %param.10) | data formatting | bytes 11796480 | tf_op args[2]
  53.1 35.9 %all-to-all-done = bf16[128,65,128]{2,1,0:T(8,128)(2,1)S(1)} async-done(((bf16[128,65,128]{2,1,0:T(8,128)(2,1)}), bf16[128,65,128]{2,1,0:T(8,128)(2,1)S(1)}, u32[]{:S(2)}, u32[]{:S(2)}) %all-to-all-start) | async-done | bytes 2129952 | tf_op jit(solution)/shard_map/all_to_all | solution.py:174
  89.1 0.5 fusion.11
  89.6 0.7 reshape.807.slot_ref
  90.3 0.7 reshape.808.qlen_ref
  91.0 1.6 slice.155
  92.7 44.6 %shard_map.103 = (bf16[256,32,128]{2,1,0:T(8,128)(2,1)}, f32[256,128]{1,0:T(8,128)}) custom-call(s32[256]{0:T(256)} %reshape.807.slot_ref, s32[256]{0:T(256)} %reshape.808.qlen_ref, s32[128]{0:T(128)} %len_ref.1, bf16[256,32,128]{2,1,0:T(8,128)(2,1)} %bitcast.46, bf16[128,180,128]{2,1,0:T(8,128)(2,1)} %copy.64.p_ref, bf16[128,128,180]{2,1,0:T(8,128)(2,1)} %bitcast.45), custom_call_target="tpu_custom_call" | custom-call | flops 754974720 | bytes 15990784 | tf_op jit(solution)/shard_map/pallas_call | solution.py:126
  137.2 1.0 slice_reduce_fusion
  138.2 0.1 squeeze.45
  138.4 0.2 slice_reduce_fusion.1
  138.6 0.2 slice_reduce_fusion.6
  138.8 0.2 slice_reduce_fusion.4
  139.0 1.1 fusion.10
  140.0 3.3 %pad_maximum_fusion.1 = bf16[128,65,128]{2,1,0:T(8,128)(2,1)} fusion(bf16[128,1,128]{2,1,0:T(2,128)(2,1)S(1)} %fusion.10, bf16[128,64,128]{2,1,0:T(8,128)(2,1)} %bitcast.48), kind=kLoop, calls=%fused_computation.1 | loop fusion | flops 4259840 | bytes 4259840 | tf_op jit(solution)/shard_map/concatenate | solution.py:181
  143.3 8.2 %all-to-all-start.1 = ((bf16[128,65,128]{2,1,0:T(8,128)(2,1)}), bf16[128,65,128]{2,1,0:T(8,128)(2,1)S(1)}, u32[]{:S(2)}, u32[]{:S(2)}) async-start(bf16[128,65,128]{2,1,0:T(8,128)(2,1)} %pad_maximum_fusion.1), calls=%async_computation.1 | async-start | bytes 4718592 | tf_op jit(solution)/shard_map/all_to_all | solution.py:184
  151.7 0.6 dynamic-slice
  153.0 0.2 dynamic-update-slice.1
  153.3 56.2 %all-to-all-done.1 = bf16[128,65,128]{2,1,0:T(8,128)(2,1)S(1)} async-done(((bf16[128,65,128]{2,1,0:T(8,128)(2,1)}), bf16[128,65,128]{2,1,0:T(8,128)(2,1)S(1)}, u32[]{:S(2)}, u32[]{:S(2)}) %all-to-all-start.1) | async-done | bytes 2129952 | tf_op jit(solution)/shard_map/all_to_all | solution.py:184
  209.6 0.2 copy.66
  209.8 0.2 reshape.809
  209.9 0.2 select_reduce_fusion
  210.2 0.1 reduce_max.19
  210.3 0.2 multiply_reduce_fusion.3
  210.6 0.2 dynamic-update-slice.3
  210.8 0.2 dynamic-update-slice
  211.0 0.2 dynamic-update-slice.2
  211.2 0.2 dynamic-update-slice.4
  211.4 2.4 all-reduce.5
  213.9 0.6 subtract_add_fusion
  214.6 0.3 slice.163
  214.9 0.9 multiply_reduce_fusion
  215.9 0.3 collective-permute-start.1
  216.1 1.1 collective-permute-done.1
  217.2 0.2 multiply_reduce_fusion.1
  217.4 0.1 subtract_convert_fusion
  217.6 0.2 convolution_bitcast_fusion
  217.8 0.1 copy.68
  218.0 21.8 %all_to_all.20 = f32[128,3,128]{2,1,0:T(4,128)S(1)} all-to-all(f32[128,3,128]{2,1,0:T(4,128)S(1)} %reshape.805), channel_id=1, replica_groups=mesh['section'=2,'shard'=128] {'shard'}, dimensions={0} | all-to-all | bytes 393216 | tf_op jit(solution)/shard_map/all_to_all | solution.py:58
  239.8 0.1 reduce_sum.112
  240.0 0.7 broadcast_in_dim.220
  240.7 6.6 %all-to-all-start.3 = ((f32[128,3,128]{2,1,0:T(4,128)}), f32[128,3,128]{2,1,0:T(4,128)S(1)}, u32[]{:S(2)}, u32[]{:S(2)}) async-start(f32[128,3,128]{2,1,0:T(4,128)} %broadcast_in_dim.220), calls=%async_computation.3 | async-start | bytes 524288 | tf_op jit(solution)/shard_map/all_to_all | solution.py:60
  247.3 0.8 convolution_convert_fusion.1
  248.1 12.5 %all-to-all-done.3 = f32[128,3,128]{2,1,0:T(4,128)S(1)} async-done(((f32[128,3,128]{2,1,0:T(4,128)}), f32[128,3,128]{2,1,0:T(4,128)S(1)}, u32[]{:S(2)}, u32[]{:S(2)}) %all-to-all-start.3) | async-done | bytes 196640 | tf_op jit(solution)/shard_map/all_to_all | solution.py:60
  260.6 0.8 reshape.806
  (41 shorter events, 1.3 us)
Async XLA Ops:
  0.6 0.9 copy-start
  2.6 8.9 %collective-permute-start = (f32[4,32,128]{2,1,0:T(8,128)S(1)}, f32[4,32,128]{2,1,0:T(8,128)S(1)}, u32[]{:S(2)}, u32[]{:S(2)}) collective-permute-start(f32[4,32,128]{2,1,0:T(8,128)S(1)} %fusion.7), channel_id=1, source_target_pairs={{0,128},{128,0},{1,129},{129,1},{2,130},{130,2},{3,131},{131,3},{4... | collective-permute-start | bytes 196616 | tf_op jit(solution)/shard_map/ppermute | solution.py:53
  15.5 73.6 %all-to-all-start = ((bf16[128,65,128]{2,1,0:T(8,128)(2,1)}), bf16[128,65,128]{2,1,0:T(8,128)(2,1)S(1)}, u32[]{:S(2)}, u32[]{:S(2)}) async-start(bf16[128,65,128]{2,1,0:T(8,128)(2,1)} %pad_maximum_fusion), calls=%async_computation | async-start | bytes 4718592 | tf_op jit(solution)/shard_map/all_to_all | solution.py:174
  143.3 8.3 %copy-start.2 = (f32[4,32]{1,0:T(4,128)S(1)}, f32[4,32]{1,0:T(4,128)}, u32[]{:S(2)}) copy-start(f32[4,32]{1,0:T(4,128)} %param.15) | copy-start | bytes 1540
  143.3 8.4 %copy-start.4 = (u32[256]{0:T(256)S(1)}, u32[256]{0:T(256)}, u32[]{:S(2)}) copy-start(u32[256]{0:T(256)} %constant.67) | copy-start | bytes 3076
  143.3 9.9 %copy-start.3 = (s32[4]{0:T(128)S(1)}, s32[4]{0:T(128)}, u32[]{:S(2)}) copy-start(s32[4]{0:T(128)} %param.12) | copy-start | bytes 52
  143.3 66.1 %all-to-all-start.1 = ((bf16[128,65,128]{2,1,0:T(8,128)(2,1)}), bf16[128,65,128]{2,1,0:T(8,128)(2,1)S(1)}, u32[]{:S(2)}, u32[]{:S(2)}) async-start(bf16[128,65,128]{2,1,0:T(8,128)(2,1)} %pad_maximum_fusion.1), calls=%async_computation.1 | async-start | bytes 4718592 | tf_op jit(solution)/shard_map/all_to_all | solution.py:184
  215.8 31.5 %copy-start.1 = (bf16[384,128]{1,0:T(8,128)(2,1)S(1)}, bf16[384,128]{1,0:T(8,128)(2,1)}, u32[]{:S(2)}) copy-start(bf16[384,128]{1,0:T(8,128)(2,1)} %param.9) | copy-start | bytes 294916
  215.9 1.3 collective-permute-start.1
  240.7 19.9 %all-to-all-start.3 = ((f32[128,3,128]{2,1,0:T(4,128)}), f32[128,3,128]{2,1,0:T(4,128)S(1)}, u32[]{:S(2)}, u32[]{:S(2)}) async-start(f32[128,3,128]{2,1,0:T(4,128)} %broadcast_in_dim.220), calls=%async_computation.3 | async-start | bytes 524288 | tf_op jit(solution)/shard_map/all_to_all | solution.py:60

commit v4 on v3

--- a/solution.py
+++ b/solution.py
@@ -9,7 +9,7 @@
 EPSILON = 1e-06
 NEGATIVE = -1e30
 CAPACITY = 2
-GROUP = 16
+GROUP = 32
 
 
 def combined_all(value, axis, join):

time: 262 us -> 261 us (level)
  no operation moved by 1% of the time
where the time goes in v4:
time: 261 us; the launch traced here: 260 us
  waiting for transfers between devices  106 us (41%)
  Pallas kernels  43 us (16%)
  local copies, waits for them, and re-layouts  36.6 us (14%)
  starting transfers between devices  30.6 us (12%)
  blocking collectives  24.3 us (9%)
  other arithmetic  14.3 us (5%)
  matrix products  3.79 us (1%)
    all_to_all x1, waiting for transfers between devices, local(): got = lax.all_to_all(back, 'shard', 0, 0, tiled=True)  56.1 us
    pallas_call x1, Pallas kernels, owner_scores(): pl.pallas_call(score_kernel, grid_spec=grid_spec, out_shape=[jax.ShapeDty...  43 us
    all_to_all x1, waiting for transfers between devices, local(): recv = lax.all_to_all(payload, 'shard', 0, 0, tiled=True)  35.9 us
    unnamed x25, local copies, waits for them, and re-layouts  25.3 us
    all_to_all x1, blocking collectives, spread_sum(): summed = lax.all_to_all(pieces, axis, 0, 0, tiled=True).sum(axis=0)  21.8 us
    all_to_all x1, starting transfers between devices, local(): recv = lax.all_to_all(payload, 'shard', 0, 0, tiled=True)  15.4 us
    all_to_all x1, waiting for transfers between devices, spread_sum(): return lax.all_to_all(spread, axis, 0, 0, tiled=True).reshape(value.shape)  12.5 us
    all_to_all x1, starting transfers between devices, local(): got = lax.all_to_all(back, 'shard', 0, 0, tiled=True)  8.17 us
  transfers between devices with their start and end apart: 5, of which 4 were waited for; matrix products, arithmetic and copies ran while one was open for 13% of the time, Pallas kernels for 0%

profile of v4, /device:TPU:2, one launch (start us, length us, event | category | flops | bytes accessed | tf_op | source)
XLA Modules:
  0.0 259.8 jit_solution(7567271768620489342)
XLA Ops:
  0.6 0.9 copy-done
  1.5 1.1 fusion.7
  2.7 1.5 fusion.28
  4.2 0.5 broadcast.645
  4.7 1.3 broadcast_multiply_fusion
  6.1 0.2 reduce_window_sum.11
  6.3 0.2 select_reduce_fusion.3
  6.5 0.8 broadcast_in_dim.201
  7.3 2.6 %fusion.22 = s32[128]{0:T(128)S(1)} fusion(s32[]{:T(128)} %bitcast.3, s32[]{:T(128)} %bitcast.4, s32[]{:T(128)} %bitcast.6, s32[]{:T(128)} %bitcast.5), kind=kLoop, calls=%fused_computation.84 | loop fusion | flops 2176 | bytes 528 | tf_op jit(solution)/shard_map/gather | solution.py:169
  9.9 0.1 select_reduce_fusion.2
  10.1 0.1 reshape.798
  10.2 0.1 reshape.799
  10.4 0.2 fusion.13
  10.6 0.6 fusion.9
  11.2 0.2 and_reduce_fusion
  11.7 0.8 convolution_convert_fusion
  12.5 1.4 copy.62
  13.8 1.7 pad_maximum_fusion
  15.5 15.4 %all-to-all-start = ((bf16[128,65,128]{2,1,0:T(8,128)(2,1)}), bf16[128,65,128]{2,1,0:T(8,128)(2,1)S(1)}, u32[]{:S(2)}, u32[]{:S(2)}) async-start(bf16[128,65,128]{2,1,0:T(8,128)(2,1)} %pad_maximum_fusion), calls=%async_computation | async-start | bytes 4718592 | tf_op jit(solution)/shard_map/all_to_all | solution.py:174
  31.0 13.1 %copy.63 = bf16[128,180,128]{1,2,0:T(8,128)(2,1)} copy(bf16[128,180,128]{2,0,1:T(8,128)(2,1)} %param.10) | data formatting | bytes 11796480 | tf_op args[2]
  44.0 9.1 %copy.64.p_ref = bf16[128,180,128]{2,1,0:T(8,128)(2,1)} copy(bf16[128,180,128]{2,0,1:T(8,128)(2,1)} %param.10) | data formatting | bytes 11796480 | tf_op args[2]
  53.1 35.9 %all-to-all-done = bf16[128,65,128]{2,1,0:T(8,128)(2,1)S(1)} async-done(((bf16[128,65,128]{2,1,0:T(8,128)(2,1)}), bf16[128,65,128]{2,1,0:T(8,128)(2,1)S(1)}, u32[]{:S(2)}, u32[]{:S(2)}) %all-to-all-start) | async-done | bytes 2129952 | tf_op jit(solution)/shard_map/all_to_all | solution.py:174
  89.1 0.5 fusion.11
  89.6 0.7 reshape.807.slot_ref
  90.3 0.7 reshape.808.qlen_ref
  91.0 1.6 slice.155
  92.7 43.0 %shard_map.103 = (bf16[256,32,128]{2,1,0:T(8,128)(2,1)}, f32[256,128]{1,0:T(8,128)}) custom-call(s32[256]{0:T(256)} %reshape.807.slot_ref, s32[256]{0:T(256)} %reshape.808.qlen_ref, s32[128]{0:T(128)} %len_ref.1, bf16[256,32,128]{2,1,0:T(8,128)(2,1)} %bitcast.46, bf16[128,180,128]{2,1,0:T(8,128)(2,1)} %copy.64.p_ref, bf16[128,128,180]{2,1,0:T(8,128)(2,1)} %bitcast.45), custom_call_target="tpu_custom_call" | custom-call | flops 754974720 | bytes 15990784 | tf_op jit(solution)/shard_map/pallas_call | solution.py:126
  135.7 1.0 slice_reduce_fusion
  136.7 0.1 squeeze.45
  136.8 0.2 slice_reduce_fusion.1
  137.0 0.2 slice_reduce_fusion.6
  137.2 0.2 slice_reduce_fusion.4
  137.4 1.1 fusion.10
  138.5 3.3 %pad_maximum_fusion.1 = bf16[128,65,128]{2,1,0:T(8,128)(2,1)} fusion(bf16[128,1,128]{2,1,0:T(2,128)(2,1)S(1)} %fusion.10, bf16[128,64,128]{2,1,0:T(8,128)(2,1)} %bitcast.48), kind=kLoop, calls=%fused_computation.1 | loop fusion | flops 4259840 | bytes 4259840 | tf_op jit(solution)/shard_map/concatenate | solution.py:181
  141.7 8.2 %all-to-all-start.1 = ((bf16[128,65,128]{2,1,0:T(8,128)(2,1)}), bf16[128,65,128]{2,1,0:T(8,128)(2,1)S(1)}, u32[]{:S(2)}, u32[]{:S(2)}) async-start(bf16[128,65,128]{2,1,0:T(8,128)(2,1)} %pad_maximum_fusion.1), calls=%async_computation.1 | async-start | bytes 4718592 | tf_op jit(solution)/shard_map/all_to_all | solution.py:184
  150.1 0.6 dynamic-slice
  151.4 0.2 dynamic-update-slice.1
  151.7 56.1 %all-to-all-done.1 = bf16[128,65,128]{2,1,0:T(8,128)(2,1)S(1)} async-done(((bf16[128,65,128]{2,1,0:T(8,128)(2,1)}), bf16[128,65,128]{2,1,0:T(8,128)(2,1)S(1)}, u32[]{:S(2)}, u32[]{:S(2)}) %all-to-all-start.1) | async-done | bytes 2129952 | tf_op jit(solution)/shard_map/all_to_all | solution.py:184
  208.0 0.2 copy.66
  208.2 0.2 reshape.809
  208.3 0.2 select_reduce_fusion
  208.6 0.1 reduce_max.19
  208.7 0.2 multiply_reduce_fusion.3
  209.0 0.2 dynamic-update-slice.3
  209.2 0.2 dynamic-update-slice
  209.4 0.2 dynamic-update-slice.2
  209.6 0.2 dynamic-update-slice.4
  209.8 2.4 all-reduce.5
  212.3 0.6 subtract_add_fusion
  213.0 0.3 slice.163
  213.3 0.9 multiply_reduce_fusion
  214.3 0.3 collective-permute-start.1
  214.5 1.1 collective-permute-done.1
  215.6 0.2 multiply_reduce_fusion.1
  215.8 0.1 subtract_convert_fusion
  215.9 0.2 convolution_bitcast_fusion
  216.2 0.1 copy.68
  216.4 21.8 %all_to_all.20 = f32[128,3,128]{2,1,0:T(4,128)S(1)} all-to-all(f32[128,3,128]{2,1,0:T(4,128)S(1)} %reshape.805), channel_id=1, replica_groups=mesh['section'=2,'shard'=128] {'shard'}, dimensions={0} | all-to-all | bytes 393216 | tf_op jit(solution)/shard_map/all_to_all | solution.py:58
  238.2 0.1 reduce_sum.112
  238.3 0.7 broadcast_in_dim.220
  239.1 6.6 %all-to-all-start.3 = ((f32[128,3,128]{2,1,0:T(4,128)}), f32[128,3,128]{2,1,0:T(4,128)S(1)}, u32[]{:S(2)}, u32[]{:S(2)}) async-start(f32[128,3,128]{2,1,0:T(4,128)} %broadcast_in_dim.220), calls=%async_computation.3 | async-start | bytes 524288 | tf_op jit(solution)/shard_map/all_to_all | solution.py:60
  245.7 0.8 convolution_convert_fusion.1
  246.5 12.5 %all-to-all-done.3 = f32[128,3,128]{2,1,0:T(4,128)S(1)} async-done(((f32[128,3,128]{2,1,0:T(4,128)}), f32[128,3,128]{2,1,0:T(4,128)S(1)}, u32[]{:S(2)}, u32[]{:S(2)}) %all-to-all-start.3) | async-done | bytes 196640 | tf_op jit(solution)/shard_map/all_to_all | solution.py:60
  259.0 0.8 reshape.806
  (41 shorter events, 1.3 us)
Async XLA Ops:
  0.6 0.9 copy-start
  2.6 8.9 %collective-permute-start = (f32[4,32,128]{2,1,0:T(8,128)S(1)}, f32[4,32,128]{2,1,0:T(8,128)S(1)}, u32[]{:S(2)}, u32[]{:S(2)}) collective-permute-start(f32[4,32,128]{2,1,0:T(8,128)S(1)} %fusion.7), channel_id=1, source_target_pairs={{0,128},{128,0},{1,129},{129,1},{2,130},{130,2},{3,131},{131,3},{4... | collective-permute-start | bytes 196616 | tf_op jit(solution)/shard_map/ppermute | solution.py:53
  15.5 73.6 %all-to-all-start = ((bf16[128,65,128]{2,1,0:T(8,128)(2,1)}), bf16[128,65,128]{2,1,0:T(8,128)(2,1)S(1)}, u32[]{:S(2)}, u32[]{:S(2)}) async-start(bf16[128,65,128]{2,1,0:T(8,128)(2,1)} %pad_maximum_fusion), calls=%async_computation | async-start | bytes 4718592 | tf_op jit(solution)/shard_map/all_to_all | solution.py:174
  141.7 8.3 %copy-start.2 = (f32[4,32]{1,0:T(4,128)S(1)}, f32[4,32]{1,0:T(4,128)}, u32[]{:S(2)}) copy-start(f32[4,32]{1,0:T(4,128)} %param.15) | copy-start | bytes 1540
  141.7 8.4 %copy-start.4 = (u32[256]{0:T(256)S(1)}, u32[256]{0:T(256)}, u32[]{:S(2)}) copy-start(u32[256]{0:T(256)} %constant.67) | copy-start | bytes 3076
  141.7 9.9 %copy-start.3 = (s32[4]{0:T(128)S(1)}, s32[4]{0:T(128)}, u32[]{:S(2)}) copy-start(s32[4]{0:T(128)} %param.12) | copy-start | bytes 52
  141.7 66.1 %all-to-all-start.1 = ((bf16[128,65,128]{2,1,0:T(8,128)(2,1)}), bf16[128,65,128]{2,1,0:T(8,128)(2,1)S(1)}, u32[]{:S(2)}, u32[]{:S(2)}) async-start(bf16[128,65,128]{2,1,0:T(8,128)(2,1)} %pad_maximum_fusion.1), calls=%async_computation.1 | async-start | bytes 4718592 | tf_op jit(solution)/shard_map/all_to_all | solution.py:184
  214.2 31.5 %copy-start.1 = (bf16[384,128]{1,0:T(8,128)(2,1)S(1)}, bf16[384,128]{1,0:T(8,128)(2,1)}, u32[]{:S(2)}) copy-start(bf16[384,128]{1,0:T(8,128)(2,1)} %param.9) | copy-start | bytes 294916
  214.3 1.3 collective-permute-start.1
  239.1 19.9 %all-to-all-start.3 = ((f32[128,3,128]{2,1,0:T(4,128)}), f32[128,3,128]{2,1,0:T(4,128)S(1)}, u32[]{:S(2)}, u32[]{:S(2)}) async-start(f32[128,3,128]{2,1,0:T(4,128)} %broadcast_in_dim.220), calls=%async_computation.3 | async-start | bytes 524288 | tf_op jit(solution)/shard_map/all_to_all | solution.py:60

commit v5 on v4

--- a/solution.py
+++ b/solution.py
@@ -9,7 +9,7 @@
 EPSILON = 1e-06
 NEGATIVE = -1e30
 CAPACITY = 2
-GROUP = 32
+GROUP = 64
 
 
 def combined_all(value, axis, join):

time: 261 us -> 260 us (level)
  no operation moved by 1% of the time
where the time goes in v5:
time: 260 us; the launch traced here: 259 us
  waiting for transfers between devices  106 us (41%)
  Pallas kernels  42.4 us (16%)
  local copies, waits for them, and re-layouts  36.6 us (14%)
  starting transfers between devices  30.5 us (12%)
  blocking collectives  24.3 us (9%)
  other arithmetic  14.3 us (6%)
  matrix products  3.79 us (1%)
    all_to_all x1, waiting for transfers between devices, local(): got = lax.all_to_all(back, 'shard', 0, 0, tiled=True)  56.2 us
    pallas_call x1, Pallas kernels, owner_scores(): pl.pallas_call(score_kernel, grid_spec=grid_spec, out_shape=[jax.ShapeDty...  42.4 us
    all_to_all x1, waiting for transfers between devices, local(): recv = lax.all_to_all(payload, 'shard', 0, 0, tiled=True)  35.9 us
    unnamed x25, local copies, waits for them, and re-layouts  25.3 us
    all_to_all x1, blocking collectives, spread_sum(): summed = lax.all_to_all(pieces, axis, 0, 0, tiled=True).sum(axis=0)  21.8 us
    all_to_all x1, starting transfers between devices, local(): recv = lax.all_to_all(payload, 'shard', 0, 0, tiled=True)  15.4 us
    all_to_all x1, waiting for transfers between devices, spread_sum(): return lax.all_to_all(spread, axis, 0, 0, tiled=True).reshape(value.shape)  12.5 us
    all_to_all x1, starting transfers between devices, local(): got = lax.all_to_all(back, 'shard', 0, 0, tiled=True)  8.12 us
  transfers between devices with their start and end apart: 5, of which 4 were waited for; matrix products, arithmetic and copies ran while one was open for 13% of the time, Pallas kernels for 0%

profile of v5, /device:TPU:2, one launch (start us, length us, event | category | flops | bytes accessed | tf_op | source)
XLA Modules:
  0.0 259.2 jit_solution(15137332713908548226)
XLA Ops:
  0.6 0.9 copy-done
  1.5 1.1 fusion.7
  2.7 1.5 fusion.28
  4.2 0.5 broadcast.645
  4.7 1.3 broadcast_multiply_fusion
  6.1 0.2 reduce_window_sum.11
  6.3 0.2 select_reduce_fusion.3
  6.5 0.8 broadcast_in_dim.201
  7.3 2.6 %fusion.22 = s32[128]{0:T(128)S(1)} fusion(s32[]{:T(128)} %bitcast.3, s32[]{:T(128)} %bitcast.4, s32[]{:T(128)} %bitcast.6, s32[]{:T(128)} %bitcast.5), kind=kLoop, calls=%fused_computation.84 | loop fusion | flops 2176 | bytes 528 | tf_op jit(solution)/shard_map/gather | solution.py:169
  9.9 0.1 select_reduce_fusion.2
  10.1 0.1 reshape.798
  10.2 0.1 reshape.799
  10.4 0.2 fusion.13
  10.6 0.6 fusion.9
  11.2 0.2 and_reduce_fusion
  11.7 0.8 convolution_convert_fusion
  12.5 1.4 copy.62
  13.8 1.7 pad_maximum_fusion
  15.5 15.4 %all-to-all-start = ((bf16[128,65,128]{2,1,0:T(8,128)(2,1)}), bf16[128,65,128]{2,1,0:T(8,128)(2,1)S(1)}, u32[]{:S(2)}, u32[]{:S(2)}) async-start(bf16[128,65,128]{2,1,0:T(8,128)(2,1)} %pad_maximum_fusion), calls=%async_computation | async-start | bytes 4718592 | tf_op jit(solution)/shard_map/all_to_all | solution.py:174
  31.0 13.1 %copy.63 = bf16[128,180,128]{1,2,0:T(8,128)(2,1)} copy(bf16[128,180,128]{2,0,1:T(8,128)(2,1)} %param.10) | data formatting | bytes 11796480 | tf_op args[2]
  44.0 9.1 %copy.64.p_ref = bf16[128,180,128]{2,1,0:T(8,128)(2,1)} copy(bf16[128,180,128]{2,0,1:T(8,128)(2,1)} %param.10) | data formatting | bytes 11796480 | tf_op args[2]
  53.1 35.9 %all-to-all-done = bf16[128,65,128]{2,1,0:T(8,128)(2,1)S(1)} async-done(((bf16[128,65,128]{2,1,0:T(8,128)(2,1)}), bf16[128,65,128]{2,1,0:T(8,128)(2,1)S(1)}, u32[]{:S(2)}, u32[]{:S(2)}) %all-to-all-start) | async-done | bytes 2129952 | tf_op jit(solution)/shard_map/all_to_all | solution.py:174
  89.1 0.5 fusion.11
  89.6 0.7 reshape.807.slot_ref
  90.3 0.7 reshape.808.qlen_ref
  91.0 1.6 slice.155
  92.7 42.4 %shard_map.103 = (bf16[256,32,128]{2,1,0:T(8,128)(2,1)}, f32[256,128]{1,0:T(8,128)}) custom-call(s32[256]{0:T(256)} %reshape.807.slot_ref, s32[256]{0:T(256)} %reshape.808.qlen_ref, s32[128]{0:T(128)} %len_ref.1, bf16[256,32,128]{2,1,0:T(8,128)(2,1)} %bitcast.46, bf16[128,180,128]{2,1,0:T(8,128)(2,1)} %copy.64.p_ref, bf16[128,128,180]{2,1,0:T(8,128)(2,1)} %bitcast.45), custom_call_target="tpu_custom_call" | custom-call | flops 754974720 | bytes 15990784 | tf_op jit(solution)/shard_map/pallas_call | solution.py:126
  135.1 1.0 slice_reduce_fusion
  136.1 0.1 squeeze.45
  136.3 0.2 slice_reduce_fusion.1
  136.5 0.2 slice_reduce_fusion.6
  136.7 0.2 slice_reduce_fusion.4
  136.8 1.1 fusion.10
  137.9 3.3 %pad_maximum_fusion.1 = bf16[128,65,128]{2,1,0:T(8,128)(2,1)} fusion(bf16[128,1,128]{2,1,0:T(2,128)(2,1)S(1)} %fusion.10, bf16[128,64,128]{2,1,0:T(8,128)(2,1)} %bitcast.48), kind=kLoop, calls=%fused_computation.1 | loop fusion | flops 4259840 | bytes 4259840 | tf_op jit(solution)/shard_map/concatenate | solution.py:181
  141.2 8.1 %all-to-all-start.1 = ((bf16[128,65,128]{2,1,0:T(8,128)(2,1)}), bf16[128,65,128]{2,1,0:T(8,128)(2,1)S(1)}, u32[]{:S(2)}, u32[]{:S(2)}) async-start(bf16[128,65,128]{2,1,0:T(8,128)(2,1)} %pad_maximum_fusion.1), calls=%async_computation.1 | async-start | bytes 4718592 | tf_op jit(solution)/shard_map/all_to_all | solution.py:184
  149.5 0.6 dynamic-slice
  150.8 0.2 dynamic-update-slice.1
  151.1 56.2 %all-to-all-done.1 = bf16[128,65,128]{2,1,0:T(8,128)(2,1)S(1)} async-done(((bf16[128,65,128]{2,1,0:T(8,128)(2,1)}), bf16[128,65,128]{2,1,0:T(8,128)(2,1)S(1)}, u32[]{:S(2)}, u32[]{:S(2)}) %all-to-all-start.1) | async-done | bytes 2129952 | tf_op jit(solution)/shard_map/all_to_all | solution.py:184
  207.4 0.2 copy.66
  207.6 0.2 reshape.809
  207.8 0.2 select_reduce_fusion
  208.1 0.1 reduce_max.19
  208.2 0.2 multiply_reduce_fusion.3
  208.4 0.2 dynamic-update-slice.3
  208.7 0.2 dynamic-update-slice
  208.9 0.2 dynamic-update-slice.2
  209.1 0.2 dynamic-update-slice.4
  209.3 2.4 all-reduce.5
  211.7 0.6 subtract_add_fusion
  212.4 0.3 slice.163
  212.7 0.9 multiply_reduce_fusion
  213.7 0.3 collective-permute-start.1
  214.0 1.1 collective-permute-done.1
  215.1 0.2 multiply_reduce_fusion.1
  215.3 0.1 subtract_convert_fusion
  215.4 0.2 convolution_bitcast_fusion
  215.6 0.1 copy.68
  215.8 21.8 %all_to_all.20 = f32[128,3,128]{2,1,0:T(4,128)S(1)} all-to-all(f32[128,3,128]{2,1,0:T(4,128)S(1)} %reshape.805), channel_id=1, replica_groups=mesh['section'=2,'shard'=128] {'shard'}, dimensions={0} | all-to-all | bytes 393216 | tf_op jit(solution)/shard_map/all_to_all | solution.py:58
  237.7 0.1 reduce_sum.112
  237.8 0.7 broadcast_in_dim.220
  238.5 6.6 %all-to-all-start.3 = ((f32[128,3,128]{2,1,0:T(4,128)}), f32[128,3,128]{2,1,0:T(4,128)S(1)}, u32[]{:S(2)}, u32[]{:S(2)}) async-start(f32[128,3,128]{2,1,0:T(4,128)} %broadcast_in_dim.220), calls=%async_computation.3 | async-start | bytes 524288 | tf_op jit(solution)/shard_map/all_to_all | solution.py:60
  245.1 0.8 convolution_convert_fusion.1
  246.0 12.5 %all-to-all-done.3 = f32[128,3,128]{2,1,0:T(4,128)S(1)} async-done(((f32[128,3,128]{2,1,0:T(4,128)}), f32[128,3,128]{2,1,0:T(4,128)S(1)}, u32[]{:S(2)}, u32[]{:S(2)}) %all-to-all-start.3) | async-done | bytes 196640 | tf_op jit(solution)/shard_map/all_to_all | solution.py:60
  258.5 0.8 reshape.806
  (41 shorter events, 1.3 us)
Async XLA Ops:
  0.6 0.9 copy-start
  2.6 8.9 %collective-permute-start = (f32[4,32,128]{2,1,0:T(8,128)S(1)}, f32[4,32,128]{2,1,0:T(8,128)S(1)}, u32[]{:S(2)}, u32[]{:S(2)}) collective-permute-start(f32[4,32,128]{2,1,0:T(8,128)S(1)} %fusion.7), channel_id=1, source_target_pairs={{0,128},{128,0},{1,129},{129,1},{2,130},{130,2},{3,131},{131,3},{4... | collective-permute-start | bytes 196616 | tf_op jit(solution)/shard_map/ppermute | solution.py:53
  15.5 73.6 %all-to-all-start = ((bf16[128,65,128]{2,1,0:T(8,128)(2,1)}), bf16[128,65,128]{2,1,0:T(8,128)(2,1)S(1)}, u32[]{:S(2)}, u32[]{:S(2)}) async-start(bf16[128,65,128]{2,1,0:T(8,128)(2,1)} %pad_maximum_fusion), calls=%async_computation | async-start | bytes 4718592 | tf_op jit(solution)/shard_map/all_to_all | solution.py:174
  141.2 8.2 %copy-start.2 = (f32[4,32]{1,0:T(4,128)S(1)}, f32[4,32]{1,0:T(4,128)}, u32[]{:S(2)}) copy-start(f32[4,32]{1,0:T(4,128)} %param.15) | copy-start | bytes 1540
  141.2 8.3 %copy-start.4 = (u32[256]{0:T(256)S(1)}, u32[256]{0:T(256)}, u32[]{:S(2)}) copy-start(u32[256]{0:T(256)} %constant.67) | copy-start | bytes 3076
  141.2 9.8 %copy-start.3 = (s32[4]{0:T(128)S(1)}, s32[4]{0:T(128)}, u32[]{:S(2)}) copy-start(s32[4]{0:T(128)} %param.12) | copy-start | bytes 52
  141.2 66.1 %all-to-all-start.1 = ((bf16[128,65,128]{2,1,0:T(8,128)(2,1)}), bf16[128,65,128]{2,1,0:T(8,128)(2,1)S(1)}, u32[]{:S(2)}, u32[]{:S(2)}) async-start(bf16[128,65,128]{2,1,0:T(8,128)(2,1)} %pad_maximum_fusion.1), calls=%async_computation.1 | async-start | bytes 4718592 | tf_op jit(solution)/shard_map/all_to_all | solution.py:184
  213.6 31.5 %copy-start.1 = (bf16[384,128]{1,0:T(8,128)(2,1)S(1)}, bf16[384,128]{1,0:T(8,128)(2,1)}, u32[]{:S(2)}) copy-start(bf16[384,128]{1,0:T(8,128)(2,1)} %param.9) | copy-start | bytes 294916
  213.7 1.3 collective-permute-start.1
  238.5 19.9 %all-to-all-start.3 = ((f32[128,3,128]{2,1,0:T(4,128)}), f32[128,3,128]{2,1,0:T(4,128)S(1)}, u32[]{:S(2)}, u32[]{:S(2)}) async-start(f32[128,3,128]{2,1,0:T(4,128)} %broadcast_in_dim.220), calls=%async_computation.3 | async-start | bytes 524288 | tf_op jit(solution)/shard_map/all_to_all | solution.py:60

commit v6 on v5

--- a/solution.py
+++ b/solution.py
@@ -13,11 +13,8 @@
 
 
 def combined_all(value, axis, join):
-    pieces = jax.tree.map(lambda part: lax.all_gather(part, axis), value)
-    head = jax.tree.map(lambda part: part[0], pieces)
-    tail = jax.tree.map(lambda part: part[1:], pieces)
-    running, _ = lax.scan(lambda running, section: (join(running, section), None), head, tail)
-    return running
+    other = lax.ppermute(jnp.stack(value), axis, [(0, 1), (1, 0)])
+    return join(value, tuple(other[place] for place in range(len(value))))
 
 
 def token_scores(q_rows, blocks, cand_lens):

time: 260 us -> 258 us (level)
    unnamed x25 -> x12, local copies, waits for them, and re-layouts: 25.3 us -> 23.7 us
  transfers between devices with their start and end apart: 5 -> 6, of which waited for: 4 -> 5; matrix products, arithmetic and copies ran while one was open for 13% -> 13% of each run, Pallas kernels for 0% -> 0%
where the time goes in v6:
time: 258 us; the launch traced here: 257 us
  waiting for transfers between devices  108 us (42%)
  Pallas kernels  42.4 us (16%)
  local copies, waits for them, and re-layouts  34.9 us (14%)
  starting transfers between devices  30.6 us (12%)
  blocking collectives  21.8 us (8%)
  other arithmetic  14.3 us (6%)
  matrix products  3.78 us (1%)
    all_to_all x1, waiting for transfers between devices, local(): got = lax.all_to_all(back, 'shard', 0, 0, tiled=True)  57.7 us
    pallas_call x1, Pallas kernels, owner_scores(): pl.pallas_call(score_kernel, grid_spec=grid_spec, out_shape=[jax.ShapeDty...  42.4 us
    all_to_all x1, waiting for transfers between devices, local(): recv = lax.all_to_all(payload, 'shard', 0, 0, tiled=True)  35.9 us
    unnamed x12, local copies, waits for them, and re-layouts  23.7 us
    all_to_all x1, blocking collectives, spread_sum(): summed = lax.all_to_all(pieces, axis, 0, 0, tiled=True).sum(axis=0)  21.8 us
    all_to_all x1, starting transfers between devices, local(): recv = lax.all_to_all(payload, 'shard', 0, 0, tiled=True)  15.4 us
    all_to_all x1, waiting for transfers between devices, spread_sum(): return lax.all_to_all(spread, axis, 0, 0, tiled=True).reshape(value.shape)  12.5 us
    all_to_all x1, starting transfers between devices, local(): got = lax.all_to_all(back, 'shard', 0, 0, tiled=True)  8.1 us
  transfers between devices with their start and end apart: 6, of which 5 were waited for; matrix products, arithmetic and copies ran while one was open for 13% of the time, Pallas kernels for 0%

profile of v6, /device:TPU:2, one launch (start us, length us, event | category | flops | bytes accessed | tf_op | source)
XLA Modules:
  0.0 256.8 jit_solution(11938453453553362987)
XLA Ops:
  0.6 0.9 copy-done
  1.5 1.1 fusion.7
  2.6 0.1 collective-permute-start
  2.7 1.5 fusion.36
  4.2 0.5 broadcast.640
  4.7 1.3 broadcast_multiply_fusion
  6.0 0.1 reshape.782
  6.1 0.2 reduce_window_sum.11
  6.3 0.2 select_reduce_fusion.3
  6.5 0.8 broadcast_in_dim.201
  7.3 2.6 %fusion.22 = s32[128]{0:T(128)S(1)} fusion(s32[]{:T(128)} %bitcast.3, s32[]{:T(128)} %bitcast.4, s32[]{:T(128)} %bitcast.6, s32[]{:T(128)} %bitcast.5), kind=kLoop, calls=%fused_computation.84 | loop fusion | flops 2176 | bytes 528 | tf_op jit(solution)/shard_map/gather | solution.py:166
  9.9 0.1 select_reduce_fusion.2
  10.1 0.1 reshape.784
  10.2 0.1 reshape.785
  10.4 0.2 fusion.13
  10.6 0.6 fusion.9
  11.2 0.2 and_reduce_fusion
  11.5 0.1 multiply_reduce_fusion.2
  11.7 0.8 convolution_convert_fusion
  12.5 1.4 copy.62
  13.8 1.7 pad_maximum_fusion
  15.5 15.4 %all-to-all-start = ((bf16[128,65,128]{2,1,0:T(8,128)(2,1)}), bf16[128,65,128]{2,1,0:T(8,128)(2,1)S(1)}, u32[]{:S(2)}, u32[]{:S(2)}) async-start(bf16[128,65,128]{2,1,0:T(8,128)(2,1)} %pad_maximum_fusion), calls=%async_computation | async-start | bytes 4718592 | tf_op jit(solution)/shard_map/all_to_all | solution.py:171
  31.0 13.1 %copy.63 = bf16[128,180,128]{1,2,0:T(8,128)(2,1)} copy(bf16[128,180,128]{2,0,1:T(8,128)(2,1)} %param.10) | data formatting | bytes 11796480 | tf_op args[2]
  44.0 9.1 %copy.64.p_ref = bf16[128,180,128]{2,1,0:T(8,128)(2,1)} copy(bf16[128,180,128]{2,0,1:T(8,128)(2,1)} %param.10) | data formatting | bytes 11796480 | tf_op args[2]
  53.1 35.9 %all-to-all-done = bf16[128,65,128]{2,1,0:T(8,128)(2,1)S(1)} async-done(((bf16[128,65,128]{2,1,0:T(8,128)(2,1)}), bf16[128,65,128]{2,1,0:T(8,128)(2,1)S(1)}, u32[]{:S(2)}, u32[]{:S(2)}) %all-to-all-start) | async-done | bytes 2129952 | tf_op jit(solution)/shard_map/all_to_all | solution.py:171
  89.1 0.5 fusion.11
  89.6 0.7 reshape.793.slot_ref
  90.3 0.7 reshape.794.qlen_ref
  91.0 1.6 slice.125
  92.7 42.4 %shard_map.103 = (bf16[256,32,128]{2,1,0:T(8,128)(2,1)}, f32[256,128]{1,0:T(8,128)}) custom-call(s32[256]{0:T(256)} %reshape.793.slot_ref, s32[256]{0:T(256)} %reshape.794.qlen_ref, s32[128]{0:T(128)} %len_ref.1, bf16[256,32,128]{2,1,0:T(8,128)(2,1)} %bitcast.108, bf16[128,180,128]{2,1,0:T(8,128)(2,1)} %copy.64.p_ref, bf16[128,128,180]{2,1,0:T(8,128)(2,1)} %bitcast.107), custom_call_target="tpu_custom_call" | custom-call | flops 754974720 | bytes 15990784 | tf_op jit(solution)/shard_map/pallas_call | solution.py:123
  135.1 1.0 slice_reduce_fusion
  136.1 0.1 squeeze.24
  136.3 0.2 slice_reduce_fusion.1
  136.4 0.2 slice_reduce_fusion.6
  136.6 0.2 slice_reduce_fusion.4
  136.8 1.1 fusion.10
  137.9 3.3 %pad_maximum_fusion.1 = bf16[128,65,128]{2,1,0:T(8,128)(2,1)} fusion(bf16[128,1,128]{2,1,0:T(2,128)(2,1)S(1)} %fusion.10, bf16[128,64,128]{2,1,0:T(8,128)(2,1)} %bitcast.110), kind=kLoop, calls=%fused_computation.1 | loop fusion | flops 4259840 | bytes 4259840 | tf_op jit(solution)/shard_map/concatenate | solution.py:178
  141.2 8.1 %all-to-all-start.1 = ((bf16[128,65,128]{2,1,0:T(8,128)(2,1)}), bf16[128,65,128]{2,1,0:T(8,128)(2,1)S(1)}, u32[]{:S(2)}, u32[]{:S(2)}) async-start(bf16[128,65,128]{2,1,0:T(8,128)(2,1)} %pad_maximum_fusion.1), calls=%async_computation.1 | async-start | bytes 4718592 | tf_op jit(solution)/shard_map/all_to_all | solution.py:181
  149.3 0.1 reduce_max.18
  149.6 57.7 %all-to-all-done.1 = bf16[128,65,128]{2,1,0:T(8,128)(2,1)S(1)} async-done(((bf16[128,65,128]{2,1,0:T(8,128)(2,1)}), bf16[128,65,128]{2,1,0:T(8,128)(2,1)S(1)}, u32[]{:S(2)}, u32[]{:S(2)}) %all-to-all-start.1) | async-done | bytes 2129952 | tf_op jit(solution)/shard_map/all_to_all | solution.py:181
  207.3 0.1 copy.70
  207.4 0.2 copy.66
  207.6 0.2 reshape.795
  207.7 0.2 select_reduce_fusion
  208.0 0.1 reduce_max.19
  208.1 0.2 multiply_reduce_fusion.3
  208.4 0.1 collective-permute-start.1
  208.5 0.3 slice.133
  208.8 0.9 collective-permute-done.1
  209.7 0.5 subtract_add_fusion
  210.3 0.9 multiply_reduce_fusion
  211.3 0.3 collective-permute-start.2
  211.6 1.1 collective-permute-done.2
  212.6 0.2 multiply_reduce_fusion.1
  212.8 0.1 subtract_convert_fusion
  213.0 0.2 convolution_bitcast_fusion
  213.2 0.1 copy.68
  213.4 21.8 %all_to_all.20 = f32[128,3,128]{2,1,0:T(4,128)S(1)} all-to-all(f32[128,3,128]{2,1,0:T(4,128)S(1)} %reshape.791), channel_id=1, replica_groups=mesh['section'=2,'shard'=128] {'shard'}, dimensions={0} | all-to-all | bytes 393216 | tf_op jit(solution)/shard_map/all_to_all | solution.py:55
  235.2 0.1 reduce_sum.112
  235.4 0.7 broadcast_in_dim.220
  236.1 6.6 %all-to-all-start.3 = ((f32[128,3,128]{2,1,0:T(4,128)}), f32[128,3,128]{2,1,0:T(4,128)S(1)}, u32[]{:S(2)}, u32[]{:S(2)}) async-start(f32[128,3,128]{2,1,0:T(4,128)} %broadcast_in_dim.220), calls=%async_computation.3 | async-start | bytes 524288 | tf_op jit(solution)/shard_map/all_to_all | solution.py:57
  242.7 0.8 convolution_convert_fusion.1
  243.5 12.5 %all-to-all-done.3 = f32[128,3,128]{2,1,0:T(4,128)S(1)} async-done(((f32[128,3,128]{2,1,0:T(4,128)}), f32[128,3,128]{2,1,0:T(4,128)S(1)}, u32[]{:S(2)}, u32[]{:S(2)}) %all-to-all-start.3) | async-done | bytes 196640 | tf_op jit(solution)/shard_map/all_to_all | solution.py:57
  256.0 0.8 reshape.792
  (31 shorter events, 0.9 us)
Async XLA Ops:
  0.6 0.9 copy-start
  2.6 8.9 %collective-permute-start = (f32[4,32,128]{2,1,0:T(8,128)S(1)}, f32[4,32,128]{2,1,0:T(8,128)S(1)}, u32[]{:S(2)}, u32[]{:S(2)}) collective-permute-start(f32[4,32,128]{2,1,0:T(8,128)S(1)} %fusion.7), channel_id=1, source_target_pairs={{0,128},{128,0},{1,129},{129,1},{2,130},{130,2},{3,131},{131,3},{4... | collective-permute-start | bytes 196616 | tf_op jit(solution)/shard_map/ppermute | solution.py:50
  15.5 73.6 %all-to-all-start = ((bf16[128,65,128]{2,1,0:T(8,128)(2,1)}), bf16[128,65,128]{2,1,0:T(8,128)(2,1)S(1)}, u32[]{:S(2)}, u32[]{:S(2)}) async-start(bf16[128,65,128]{2,1,0:T(8,128)(2,1)} %pad_maximum_fusion), calls=%async_computation | async-start | bytes 4718592 | tf_op jit(solution)/shard_map/all_to_all | solution.py:171
  141.1 8.2 %copy-start.2 = (f32[4,32]{1,0:T(4,128)S(1)}, f32[4,32]{1,0:T(4,128)}, u32[]{:S(2)}) copy-start(f32[4,32]{1,0:T(4,128)} %param.15) | copy-start | bytes 1540
  141.2 8.3 %copy-start.3 = (s32[4]{0:T(128)S(1)}, s32[4]{0:T(128)}, u32[]{:S(2)}) copy-start(s32[4]{0:T(128)} %param.12) | copy-start | bytes 52
  141.2 66.1 %all-to-all-start.1 = ((bf16[128,65,128]{2,1,0:T(8,128)(2,1)}), bf16[128,65,128]{2,1,0:T(8,128)(2,1)S(1)}, u32[]{:S(2)}, u32[]{:S(2)}) async-start(bf16[128,65,128]{2,1,0:T(8,128)(2,1)} %pad_maximum_fusion.1), calls=%async_computation.1 | async-start | bytes 4718592 | tf_op jit(solution)/shard_map/all_to_all | solution.py:181
  208.4 1.3 collective-permute-start.1
  211.2 31.5 %copy-start.1 = (bf16[384,128]{1,0:T(8,128)(2,1)S(1)}, bf16[384,128]{1,0:T(8,128)(2,1)}, u32[]{:S(2)}) copy-start(bf16[384,128]{1,0:T(8,128)(2,1)} %param.9) | copy-start | bytes 294916
  211.3 1.3 collective-permute-start.2
  236.1 19.9 %all-to-all-start.3 = ((f32[128,3,128]{2,1,0:T(4,128)}), f32[128,3,128]{2,1,0:T(4,128)S(1)}, u32[]{:S(2)}, u32[]{:S(2)}) async-start(f32[128,3,128]{2,1,0:T(4,128)} %broadcast_in_dim.220), calls=%async_computation.3 | async-start | bytes 524288 | tf_op jit(solution)/shard_map/all_to_all | solution.py:57
